TPU v7x, 256 devices: a whole 4x4x8 slice. The times are simulated.
256 devices in a mesh: blk: 8 (over x, core), dev: 32 (over z, y).
Axes of the slice: x: 4, y: 4, z: 8, core: 2. Of those that a mesh axis runs over, the one named last changes fastest.
Arguments:
- echoes: bfloat16 [2, 4, 2048, 16384], P(None, None, ('blk', 'dev')), may hold values from -6 to 6
- range_phase: float32 [16384], replicated, may hold values from -3.140625 to 3.140625
- offsets: int32 [16384], P('dev'), may hold values from 0 to 56, as said below
- tap_weights: float32 [8, 384], replicated, may hold values from -2 to 2
- channel_mix: float32 [2, 4, 4, 384], replicated, may hold values from -2 to 2
- azimuth_filter: float32 [2, 4, 384], replicated, may hold values from -4 to 4
Outputs:
- focused_image: bfloat16 [2, 4, 2048, 16384], P(None, None, 'blk', 'dev')
Inputs may be any that keep to these rules, and one draw needn't show every extreme that they name: `offsets`: each range bin's offset lies between 0 and 56; some range bin has exactly 56.
All inputs are finite; a program needn't handle non-finite values.
Results may differ from a plain program's by a relative error of at most 0.0088.
Values may be sent and summed in bfloat16 or wider, within the bound.
No kernel may reach another device: no remote copies, remote signals or barrier semaphores. Data moves between devices by JAX's collectives and lax.ppermute only.
A program may use at most 128 MiB of HBM per device.

v0:
```python
import math

import jax
import jax.numpy as jnp
from jax import lax
from jax.sharding import PartitionSpec as P

R1 = 128
MARG = 64


def shifted(block, axis, distance):
    devices = range(lax.axis_size(axis))
    route = [(i - distance, i) for i in devices if i - distance in devices]
    return lax.ppermute(block, axis, route)


def phase_pair(row_count, col_count, length, direction, factor):
    product = (
        jnp.arange(row_count, dtype=jnp.int32)[:, None]
        * jnp.arange(col_count, dtype=jnp.int32)[None, :]
        % length
    )
    angle = product.astype(jnp.float32) * (direction * 2.0 * math.pi / length)
    return (jnp.cos(angle) * factor, jnp.sin(angle) * factor)


def complex_table(row_count, col_count, length, direction, factor):
    cosine, sine = phase_pair(row_count, col_count, length, direction, factor)
    upper = jnp.stack([cosine, -sine], axis=1)
    lower = jnp.stack([sine, cosine], axis=1)
    return jnp.stack([upper, lower]).astype(jnp.bfloat16)


def apply_table(table, data, part_dim, index_dim):
    return lax.dot_general(
        table, data, (((2, 3), (part_dim, index_dim)), ((), ())), preferred_element_type=jnp.float32
    )


def compress(echoes, range_phase):
    cosine = jnp.cos(range_phase)
    sine = jnp.sin(range_phase)
    real_in = echoes[0].astype(jnp.float32)
    imag_in = echoes[1].astype(jnp.float32)
    spectrum = jnp.stack(
        [real_in * cosine - imag_in * sine, real_in * sine + imag_in * cosine]
    ).astype(jnp.bfloat16)
    channels = spectrum.shape[1]
    pulses = spectrum.shape[2]
    range_bins = spectrum.shape[3]
    second = range_bins // R1
    spectrum = spectrum.reshape((2, channels, pulses, R1, second))
    section = apply_table(complex_table(R1, R1, R1, 1.0, 1.0), spectrum, 0, 3)
    twist_re, twist_im = phase_pair(R1, second, range_bins, 1.0, 1.0 / math.sqrt(range_bins))
    twist_re = twist_re[:, None, None, :]
    twist_im = twist_im[:, None, None, :]
    partial_terms = jnp.stack(
        [
            section[0] * twist_re - section[1] * twist_im,
            section[0] * twist_im + section[1] * twist_re,
        ]
    ).astype(jnp.bfloat16)
    result = apply_table(
        complex_table(second, second, second, 1.0, 1.0), partial_terms, 0, 4
    ).astype(jnp.bfloat16)
    return result.transpose(0, 3, 4, 1, 2).reshape((2, channels, pulses, range_bins))


def doppler(window):
    wide = window.shape[2]
    forward = complex_table(wide, wide, wide, -1.0, 1.0 / math.sqrt(wide))
    return apply_table(forward, window, 0, 2).astype(jnp.bfloat16)


def migrate(extended, offsets, tap_weights, block):
    tile = min(128, block)
    taps = tap_weights.shape[0]
    pieces = []
    for tile_index in range(block // tile):
        first = tile_index * tile
        rows_here = jnp.arange(tile, dtype=jnp.int32)
        target = rows_here + offsets[first : first + tile]
        columns = jnp.arange(tile + MARG, dtype=jnp.int32)
        tap_range = jnp.arange(taps, dtype=jnp.int32)
        onehot = (
            columns[None, None, :] == target[None, :, None] + tap_range[:, None, None]
        ).astype(jnp.bfloat16)
        window_part = extended[:, :, :, first : first + tile + MARG]
        picked = lax.dot_general(
            window_part, onehot, (((3,), (2,)), ((), ())), preferred_element_type=jnp.float32
        )
        total = jnp.zeros(picked.shape[:3] + (tile,), jnp.float32)
        for tap_index in range(taps):
            total = total + picked[:, :, :, tap_index] * tap_weights[tap_index][None, :, None, None]
        pieces.append(total)
    return jnp.concatenate(pieces, axis=3)


def body(echoes, range_phase, offsets, tap_weights, channel_mix, azimuth_filter):
    dev_count = lax.axis_size("dev")
    compressed = compress(echoes, range_phase)
    range_bins = compressed.shape[3]
    block = range_bins // dev_count
    turned = lax.all_to_all(compressed, "dev", split_axis=3, concat_axis=2, tiled=True)
    group_pulses = turned.shape[2]
    intersection = group_pulses // 2
    following = shifted(turned[:, :, :intersection], "blk", -1)
    spectra = doppler(jnp.concatenate([turned, following], axis=2))
    border = shifted(spectra[:, :, :, :MARG], "dev", -1)
    extended = jnp.concatenate([spectra, border], axis=3)
    wide = extended.shape[1]
    channels = extended.shape[2]
    moved = migrate(extended, offsets, tap_weights, block)
    mix_real = (
        azimuth_filter[0][:, None, :] * channel_mix[0]
        - azimuth_filter[1][:, None, :] * channel_mix[1]
    )
    mix_imag = (
        azimuth_filter[0][:, None, :] * channel_mix[1]
        + azimuth_filter[1][:, None, :] * channel_mix[0]
    )
    rows_real = []
    rows_imag = []
    for channel in range(channels):
        sum_real = jnp.zeros((wide, block), jnp.float32)
        sum_imag = jnp.zeros((wide, block), jnp.float32)
        for other_chan in range(channels):
            coef_real = mix_real[channel, other_chan][:, None]
            coef_imag = mix_imag[channel, other_chan][:, None]
            sum_real = (
                sum_real + coef_real * moved[0, :, other_chan] - coef_imag * moved[1, :, other_chan]
            )
            sum_imag = (
                sum_imag + coef_real * moved[1, :, other_chan] + coef_imag * moved[0, :, other_chan]
            )
        rows_real.append(sum_real)
        rows_imag.append(sum_imag)
    focused = jnp.stack([jnp.stack(rows_real, axis=1), jnp.stack(rows_imag, axis=1)]).astype(
        jnp.bfloat16
    )
    backward = complex_table(group_pulses, wide, wide, 1.0, 1.0 / math.sqrt(wide))
    image = apply_table(backward, focused, 0, 1).astype(jnp.bfloat16)
    return image.transpose(0, 2, 1, 3)


def solution(mesh):
    in_specs = (P(None, None, ("blk", "dev"), None), P(), P("dev"), P(), P(), P())
    out_specs = P(None, None, "blk", "dev")
    return jax.shard_map(body, mesh=mesh, in_specs=in_specs, out_specs=out_specs, check_vma=False)
```

profile of v0, /device:TPU:1, one launch (start us, length us, event | category | flops | bytes accessed | tf_op | source)
XLA Modules:
  0.0 276.6 jit_solution(915196148581060619)
XLA Ops:
  0.8 1.1 fusion.138
  1.9 2.2 fusion.88
  4.1 0.6 copy_bitcast_fusion
  4.7 0.7 convolution_bitcast_fusion
  5.5 0.6 subtract_convert_fusion
  6.1 0.7 fusion.15
  6.8 24.4 %copy.105 = bf16[2,4,8,128,128]{2,1,0,4,3:T(4,128)(2,1)} copy(bf16[2,4,8,128,128]{4,3,2,1,0:T(8,128)(2,1)S(1)} %fusion.15) | data formatting | bytes 4194304 | tf_op jit(solution)/shard_map/reshape | solution.py:67
  31.2 39.5 %reshape.3041 = bf16[32,2,16384]{2,1,0:T(2,128)(2,1)} reshape(bf16[16384,2,4,8]{3,2,1,0:T(4,128)(2,1)} %bitcast.547) | data formatting | bytes 4194304
  70.8 12.2 %all-to-all-start = ((bf16[32,2,16384]{2,1,0:T(2,128)(2,1)}), bf16[32,2,16384]{2,1,0:T(2,128)(2,1)S(1)}, u32[]{:S(2)}, u32[]{:S(2)}) async-start(bf16[32,2,16384]{2,1,0:T(2,128)(2,1)} %reshape.3041), calls=%async_computation | async-start | bytes 4194304 | tf_op jit(solution)/shard_map/all_to_all | solution.py:105
  83.0 0.7 slice_reduce_fusion.30
  83.7 0.7 slice_reduce_fusion.31
  84.4 1.5 fusion.116
  85.9 2.3 fusion.106
  88.2 1.7 negate_convert_fusion.1
  90.0 2.6 negate_convert_fusion
  92.6 0.8 maximum_bitcast_fusion.16
  93.4 38.0 %all-to-all-done = bf16[32,2,16384]{2,1,0:T(2,128)(2,1)S(1)} async-done(((bf16[32,2,16384]{2,1,0:T(2,128)(2,1)}), bf16[32,2,16384]{2,1,0:T(2,128)(2,1)S(1)}, u32[]{:S(2)}, u32[]{:S(2)}) %all-to-all-start) | async-done | bytes 2097184 | tf_op jit(solution)/shard_map/all_to_all | solution.py:105
  131.4 40.6 %reshape.3042 = bf16[16384,2,4,8]{3,2,1,0:T(4,128)(2,1)} reshape(bf16[32,2,16384]{2,1,0:T(2,128)(2,1)S(1)} %all-to-all-done) | data formatting | bytes 4194304
  172.0 40.2 %copy.47 = bf16[2,4,8,32,512]{4,2,3,0,1:T(8,128)(2,1)S(1)} copy(bf16[2,4,8,32,512]{2,1,0,4,3:T(4,128)(2,1)} %bitcast.548) | data formatting | bytes 4194304 | tf_op jit(solution)/shard_map/all_to_all | solution.py:105
  212.4 4.7 %collective-permute-start = (bf16[2,4,128,512]{3,2,0,1:T(8,128)(2,1)S(1)}, bf16[2,4,128,512]{3,2,0,1:T(8,128)(2,1)S(1)}, u32[]{:S(2)}, u32[]{:S(2)}) collective-permute-start(bf16[2,4,128,512]{3,2,0,1:T(8,128)(2,1)S(1)} %slice.481), channel_id=1, source_target_pairs={{32,0},{64,32},{96,64},{128,96},{160,128},{192,160},{224,192},{33,... | collective-permute-start | bytes 3145736 | tf_op jit(solution)/shard_map/ppermute | solution.py:15
  217.1 0.6 slice_reduce_fusion.39
  218.0 0.6 iota_add_fusion.3
  218.6 11.9 %collective-permute-done = bf16[2,4,128,512]{3,2,0,1:T(8,128)(2,1)S(1)} collective-permute-done((bf16[2,4,128,512]{3,2,0,1:T(8,128)(2,1)S(1)}, bf16[2,4,128,512]{3,2,0,1:T(8,128)(2,1)S(1)}, u32[]{:S(2)}, u32[]{:S(2)}) %collective-permute-start) | collective-permute-done | bytes 1048608 | tf_op jit(solution)/shard_map/ppermute | solution.py:15
  230.5 4.4 %bitcast_convert_fusion = bf16[2,384,4,512]{3,1,2,0:T(8,128)(2,1)S(1)} fusion(bf16[2,4,128,512]{3,2,0,1:T(8,128)(2,1)S(1)} %collective-permute-done, bf16[2,4,256,512]{3,2,0,1:T(8,128)(2,1)} %bitcast.550, bf16[1,384,2,384]{3,1,2,0:T(8,128)(2,1)S(1)} %get-tuple-element.50, bf16[1,384,2,384]{3,1,2,0:T(8,128)(2,1)S(1)} %get-tuple-element.49), kind=kOutput, calls=%fused_computation.1 | convolution fusion | flops 2426142720 | bytes 7471104 | tf_op jit(solution)/shard_map/dot_general | solution.py:36
  234.9 1.0 slice.509
  235.9 2.1 copy.74
  238.1 1.3 collective-permute-start.1
  239.4 1.8 fusion.52
  241.2 1.8 fusion.68
  243.2 6.4 %fusion.84 = f32[2,384,4,8,128]{1,4,3,2,0:T(8,128)} fusion(bf16[2,384,4,512]{3,1,2,0:T(8,128)(2,1)S(1)} %bitcast_convert_fusion, s32[8,128]{1,0:T(8,128)S(1)} %copy-done.51), kind=kOutput, calls=%fused_computation.132 | convolution fusion | flops 1208156160 | bytes 14159872 | tf_op jit(solution)/shard_map/dot_general | solution.py:90
  249.6 2.3 fusion.38
  251.9 2.3 fusion.54
  254.2 2.8 %copy-done = f32[2,384,4,8,128]{1,4,3,2,0:T(8,128)S(1)} copy-done((f32[2,384,4,8,128]{1,4,3,2,0:T(8,128)S(1)}, f32[2,384,4,8,128]{1,4,3,2,0:T(8,128)}, u32[]{:S(2)}) %copy-start) | copy-done | bytes 12582936
  257.0 2.3 fusion.70
  259.3 2.2 copy.75
  261.5 3.0 %fusion.34 = f32[2,384,4,8,128]{1,4,2,0,3:T(8,128)S(1)} fusion(bf16[2,384,4,64]{3,1,2,0:T(8,128)(2,1)} %copy.75, bf16[2,384,4,512]{3,1,2,0:T(8,128)(2,1)S(1)} %bitcast_convert_fusion, s32[8,128]{1,0:T(8,128)S(1)} %iota_add_fusion), kind=kOutput, calls=%fused_computation.56 | convolution fusion | flops 1210515456 | bytes 16125952 | tf_op jit(solution)/shard_map/dot_general | solution.py:90
  264.6 1.1 fusion.19
  266.0 0.5 copy-done.2
  266.4 0.5 copy-done.3
  267.0 0.7 pad_maximum_fusion
  267.7 0.4 subtract_convert_fusion.3
  268.9 0.4 subtract_convert_fusion.4
  269.4 0.4 add_convert_fusion.4
  270.1 0.4 subtract_convert_fusion.2
  270.6 0.4 add_convert_fusion.2
  271.3 0.4 subtract_convert_fusion.1
  272.7 0.7 copy-done.5
  273.4 3.2 %fusion.10 = bf16[2,4,256,512]{3,2,1,0:T(8,128)(2,1)} fusion(bf16[1,384,4,512]{1,3,2,0:T(8,128)(2,1)S(1)} %maximum_bitcast_fusion.11, bf16[1,384,4,512]{1,3,2,0:T(8,128)(2,1)S(1)} %maximum_bitcast_fusion.10, bf16[1,256,2,384]{3,1,2,0:T(8,128)(2,1)S(1)} %copy-done.5, bf16[1,256,2,384]{3,1,2,0:T(8,128)(2,1)S(1)} %get-tuple-element.51), kind=kOutput, calls=%fused_computation.21 | convolution fusion | flops 1619525632 | bytes 6029312 | tf_op jit(solution)/shard_map/dot_general | solution.py:36
  (122 shorter events, 3.6 us)
Async XLA Ops:
  70.8 12.2 %copy-start.53 = (f32[2,4,384]{2,1,0:T(4,128)S(1)}, f32[2,4,384]{2,1,0:T(4,128)}, u32[]{:S(2)}) copy-start(f32[2,4,384]{2,1,0:T(4,128)} %param.11) | copy-start | bytes 36868
  70.8 12.2 %copy-start.18 = (f32[2,4,4,384]{3,2,1,0:T(4,128)S(1)}, f32[2,4,4,384]{3,2,1,0:T(4,128)}, u32[]{:S(2)}) copy-start(f32[2,4,4,384]{3,2,1,0:T(4,128)} %param.10) | copy-start | bytes 147460
  70.8 60.6 %all-to-all-start = ((bf16[32,2,16384]{2,1,0:T(2,128)(2,1)}), bf16[32,2,16384]{2,1,0:T(2,128)(2,1)S(1)}, u32[]{:S(2)}, u32[]{:S(2)}) async-start(bf16[32,2,16384]{2,1,0:T(2,128)(2,1)} %reshape.3041), calls=%async_computation | async-start | bytes 4194304 | tf_op jit(solution)/shard_map/all_to_all | solution.py:105
  212.3 5.6 %copy-start.4 = (bf16[2,4,8,32,512]{4,2,3,0,1:T(8,128)(2,1)}, bf16[2,4,8,32,512]{4,2,3,0,1:T(8,128)(2,1)S(1)}, u32[]{:S(2)}) copy-start(bf16[2,4,8,32,512]{4,2,3,0,1:T(8,128)(2,1)S(1)} %copy.47) | copy-start | bytes 6291460
  212.3 4.8 %copy-start.52 = (f32[8,384]{1,0:T(8,128)S(1)}, f32[8,384]{1,0:T(8,128)}, u32[]{:S(2)}) copy-start(f32[8,384]{1,0:T(8,128)} %param.9) | copy-start | bytes 36868
  212.3 5.6 %copy-start.54 = (s32[512]{0:T(512)S(1)}, s32[512]{0:T(512)}, u32[]{:S(2)}) copy-start(s32[512]{0:T(512)} %param.8) | copy-start | bytes 6148
  212.4 18.1 %collective-permute-start = (bf16[2,4,128,512]{3,2,0,1:T(8,128)(2,1)S(1)}, bf16[2,4,128,512]{3,2,0,1:T(8,128)(2,1)S(1)}, u32[]{:S(2)}, u32[]{:S(2)}) collective-permute-start(bf16[2,4,128,512]{3,2,0,1:T(8,128)(2,1)S(1)} %slice.481), channel_id=1, source_target_pairs={{32,0},{64,32},{96,64},{128,96},{160,128},{192,160},{224,192},{33,... | collective-permute-start | bytes 3145736 | tf_op jit(solution)/shard_map/ppermute | solution.py:15
  238.1 21.2 %collective-permute-start.1 = (bf16[2,384,4,64]{1,3,2,0:T(8,128)(2,1)}, bf16[2,384,4,64]{1,3,2,0:T(8,128)(2,1)}, u32[]{:S(2)}, u32[]{:S(2)}) collective-permute-start(bf16[2,384,4,64]{1,3,2,0:T(8,128)(2,1)} %copy.74), channel_id=1, source_target_pairs={{1,0},{2,1},{3,2},{4,3},{5,4},{6,5},{7,6},{8,7},{9,8},{10,9},{11,1... | collective-permute-start | bytes 1179656 | tf_op jit(solution)/shard_map/ppermute | solution.py:15
  241.2 1.9 copy-start.51
  243.1 6.5 %copy-start.6 = (f32[384]{0:T(512)S(1)}, f32[384]{0:T(512)}, u32[]{:S(2)}) copy-start(f32[384]{0:T(512)} %get-tuple-element.38) | copy-start | bytes 4612
  243.1 6.5 %copy-start.7 = (f32[384]{0:T(512)S(1)}, f32[384]{0:T(512)}, u32[]{:S(2)}) copy-start(f32[384]{0:T(512)} %get-tuple-element.39) | copy-start | bytes 4612
  243.1 6.5 %copy-start.8 = (f32[384]{0:T(512)S(1)}, f32[384]{0:T(512)}, u32[]{:S(2)}) copy-start(f32[384]{0:T(512)} %get-tuple-element.40) | copy-start | bytes 4612
  243.1 6.5 %copy-start.10 = (f32[384]{0:T(512)S(1)}, f32[384]{0:T(512)}, u32[]{:S(2)}) copy-start(f32[384]{0:T(512)} %get-tuple-element.41) | copy-start | bytes 4612
  243.1 6.5 %copy-start.12 = (f32[384]{0:T(512)S(1)}, f32[384]{0:T(512)}, u32[]{:S(2)}) copy-start(f32[384]{0:T(512)} %get-tuple-element.42) | copy-start | bytes 4612
  243.1 6.5 %copy-start.14 = (f32[384]{0:T(512)S(1)}, f32[384]{0:T(512)}, u32[]{:S(2)}) copy-start(f32[384]{0:T(512)} %get-tuple-element.43) | copy-start | bytes 4612
  243.1 6.5 %copy-start.16 = (f32[384]{0:T(512)S(1)}, f32[384]{0:T(512)}, u32[]{:S(2)}) copy-start(f32[384]{0:T(512)} %get-tuple-element.44) | copy-start | bytes 4612
  251.9 5.1 %copy-start = (f32[2,384,4,8,128]{1,4,3,2,0:T(8,128)S(1)}, f32[2,384,4,8,128]{1,4,3,2,0:T(8,128)}, u32[]{:S(2)}) copy-start(f32[2,384,4,8,128]{1,4,3,2,0:T(8,128)} %fusion.84) | copy-start | bytes 37748740
  261.5 3.0 %copy-start.9 = (f32[384]{0:T(512)S(1)}, f32[384]{0:T(512)}, u32[]{:S(2)}) copy-start(f32[384]{0:T(512)} %get-tuple-element.40) | copy-start | bytes 4612
  261.5 3.0 %copy-start.11 = (f32[384]{0:T(512)S(1)}, f32[384]{0:T(512)}, u32[]{:S(2)}) copy-start(f32[384]{0:T(512)} %get-tuple-element.41) | copy-start | bytes 4612
  261.5 3.0 %copy-start.13 = (f32[384]{0:T(512)S(1)}, f32[384]{0:T(512)}, u32[]{:S(2)}) copy-start(f32[384]{0:T(512)} %get-tuple-element.42) | copy-start | bytes 4612
  261.5 3.0 %copy-start.15 = (f32[384]{0:T(512)S(1)}, f32[384]{0:T(512)}, u32[]{:S(2)}) copy-start(f32[384]{0:T(512)} %get-tuple-element.43) | copy-start | bytes 4612
  261.5 3.0 %copy-start.17 = (f32[384]{0:T(512)S(1)}, f32[384]{0:T(512)}, u32[]{:S(2)}) copy-start(f32[384]{0:T(512)} %get-tuple-element.44) | copy-start | bytes 4612
  264.5 1.4 copy-start.1
  264.6 1.9 copy-start.2
  264.6 2.3 copy-start.3
  266.9 0.7 copy-start.35
  266.9 0.7 copy-start.36
  266.9 0.8 copy-start.37
  266.9 0.8 copy-start.38
  266.9 0.8 copy-start.47
  266.9 0.8 copy-start.48
  266.9 0.8 copy-start.49
  266.9 0.8 copy-start.50
  268.2 0.7 copy-start.27
  268.2 0.7 copy-start.29
  268.2 0.7 copy-start.30
  268.2 0.7 copy-start.43
  268.2 0.7 copy-start.44
  268.2 0.7 copy-start.45
  268.2 0.7 copy-start.46
  269.4 0.7 copy-start.23
  269.4 0.7 copy-start.24
  269.4 0.7 copy-start.39
  269.4 0.7 copy-start.41
  270.5 0.7 copy-start.19
  270.6 0.7 copy-start.20
  270.6 0.7 copy-start.34
  272.4 1.0 copy-start.5
  (10 other events, 6.7 us)
where the time goes:
time: 281 us; the launch traced here: 277 us
  local copies, waits for them, and re-layouts  159 us (57%)
  waiting for transfers between devices  50 us (18%)
  other arithmetic  26.1 us (9%)
  matrix products  22.1 us (8%)
  starting transfers between devices  18.2 us (6%)
    unnamed x112, local copies, waits for them, and re-layouts  85.8 us
    all_to_all x1, local copies, waits for them, and re-layouts, body(): lax.all_to_all(compressed, 'dev', split_axis=3, concat_axis=2, tiled=True)  40.2 us
    all_to_all x1, waiting for transfers between devices, body(): lax.all_to_all(compressed, 'dev', split_axis=3, concat_axis=2, tiled=True)  38 us
    reshape x1, local copies, waits for them, and re-layouts, compress(): result.transpose(0, 3, 4, 1, 2).reshape((2, channels, pulses, range_bins))  24.4 us
    dot_general x4, matrix products, migrate(): lax.dot_general(window_part, onehot, (((3,), (2,)), ((), ())), preferred_...  13.1 us
    another operation x15, other arithmetic  12.8 us
    all_to_all x1, starting transfers between devices, body(): lax.all_to_all(compressed, 'dev', split_axis=3, concat_axis=2, tiled=True)  12.2 us
    ppermute x2, waiting for transfers between devices, shifted(): return lax.ppermute(block, axis, route)  11.9 us
  transfers between devices with their start and end apart: 3, of which 2 were waited for; matrix products, arithmetic and copies ran while one was open for 10% of the time, Pallas kernels for 0%

commit v1 on v0

--- a/solution.py
+++ b/solution.py
@@ -99,18 +99,49 @@
 
 def body(echoes, range_phase, offsets, tap_weights, channel_mix, azimuth_filter):
     dev_count = lax.axis_size("dev")
-    compressed = compress(echoes, range_phase)
-    range_bins = compressed.shape[3]
+    parts, channels, pulses, range_bins = echoes.shape
+    second = range_bins // R1
+    per_block = second // dev_count
     block = range_bins // dev_count
-    turned = lax.all_to_all(compressed, "dev", split_axis=3, concat_axis=2, tiled=True)
-    group_pulses = turned.shape[2]
-    intersection = group_pulses // 2
-    following = shifted(turned[:, :, :intersection], "blk", -1)
-    spectra = doppler(jnp.concatenate([turned, following], axis=2))
+    cosine = jnp.cos(range_phase)
+    sine = jnp.sin(range_phase)
+    real_in = echoes[0].astype(jnp.float32)
+    imag_in = echoes[1].astype(jnp.float32)
+    spectrum = jnp.stack(
+        [real_in * cosine - imag_in * sine, real_in * sine + imag_in * cosine]
+    ).astype(jnp.bfloat16)
+    spectrum = spectrum.reshape((2, channels, pulses, R1, second))
+    section = apply_table(complex_table(R1, R1, R1, 1.0, 1.0), spectrum, 0, 3)
+    twist_re, twist_im = phase_pair(R1, second, range_bins, 1.0, 1.0 / math.sqrt(range_bins))
+    twist_re = twist_re[:, None, None, :]
+    twist_im = twist_im[:, None, None, :]
+    partial_terms = jnp.stack(
+        [
+            section[0] * twist_re - section[1] * twist_im,
+            section[0] * twist_im + section[1] * twist_re,
+        ]
+    ).astype(jnp.bfloat16)
+    partial_terms = partial_terms.transpose(0, 2, 3, 1, 4)
+    second_table = complex_table(second, second, second, 1.0, 1.0).transpose(1, 0, 2, 3)
+    second_table = second_table.reshape((dev_count, per_block, 2, 2, second))
+    result = lax.dot_general(
+        second_table, partial_terms, (((3, 4), (0, 4)), ((), ())), preferred_element_type=jnp.float32
+    ).astype(jnp.bfloat16)
+    result = result.transpose(0, 2, 3, 4, 1, 5).reshape((dev_count, 2, channels, pulses, block))
+    turned = lax.all_to_all(result, "dev", 0, 0, tiled=True)
+    group_pulses = dev_count * pulses
+    wide = group_pulses + group_pulses // 2
+    following = shifted(turned[: dev_count // 2], "blk", -1)
+    forward = complex_table(wide, wide, wide, -1.0, 1.0 / math.sqrt(wide))
+    own_table = forward[:, :, :, :group_pulses].reshape((2, wide, 2, dev_count, pulses))
+    next_table = forward[:, :, :, group_pulses:].reshape((2, wide, 2, dev_count // 2, pulses))
+    dims = (((2, 3, 4), (1, 0, 3)), ((), ()))
+    spectra = (
+        lax.dot_general(own_table, turned, dims, preferred_element_type=jnp.float32)
+        + lax.dot_general(next_table, following, dims, preferred_element_type=jnp.float32)
+    ).astype(jnp.bfloat16)
     border = shifted(spectra[:, :, :, :MARG], "dev", -1)
     extended = jnp.concatenate([spectra, border], axis=3)
-    wide = extended.shape[1]
-    channels = extended.shape[2]
     moved = migrate(extended, offsets, tap_weights, block)
     mix_real = (
         azimuth_filter[0][:, None, :] * channel_mix[0]

time: 281 us -> 134 us (0.48)
  local copies, waits for them, and re-layouts: 159 us -> 16.5 us
    unnamed x112 -> x115, local copies, waits for them, and re-layouts: 85.8 us -> 5.81 us
    all_to_all x1 -> x0, local copies, waits for them, and re-layouts: 40.2 us -> none  [body(): lax.all_to_all(compressed, 'dev', split_axis=3, concat_axis=2, tiled=True)]
    reshape x1, local copies, waits for them, and re-layouts: 24.4 us -> 1.59 us  [body(): result.transpose(0, 2, 3, 4, 1, 5)]
    dot_general x4 -> x2, matrix products: 9.04 us -> 3.87 us  [apply_table(): lax.dot_general(table, data, (((2, 3), (part_dim, index_dim)), ((), ())),...]
    dot_general x0 -> x3, matrix products: none -> 4.79 us  [the longest x1 2.14 us: body(): lax.dot_general(next_table, following, dims, preferred_element_type=jnp.f...]
  transfers between devices with their start and end apart: 3 -> 3, of which waited for: 2 -> 2; matrix products, arithmetic and copies ran while one was open for 10% -> 23% of each run, Pallas kernels for 0% -> 0%
where the time goes in v1:
time: 134 us; the launch traced here: 132 us
  waiting for transfers between devices  48.3 us (36%)
  other arithmetic  26.3 us (20%)
  matrix products  21.7 us (16%)
  starting transfers between devices  18.2 us (14%)
  local copies, waits for them, and re-layouts  16.5 us (12%)
    all_to_all x1, waiting for transfers between devices, body(): turned = lax.all_to_all(result, 'dev', 0, 0, tiled=True)  36.4 us
    dot_general x4, matrix products, migrate(): lax.dot_general(window_part, onehot, (((3,), (2,)), ((), ())), preferred_...  13.1 us
    another operation x15, other arithmetic  12.8 us
    all_to_all x1, starting transfers between devices, body(): turned = lax.all_to_all(result, 'dev', 0, 0, tiled=True)  12.2 us
    ppermute x2, waiting for transfers between devices, shifted(): return lax.ppermute(block, axis, route)  11.8 us
    add x4, other arithmetic, migrate(): total + picked[:, :, :, tap_index] * tap_weights[tap_index][None, :, None...  8 us
    ppermute x2, starting transfers between devices, shifted(): return lax.ppermute(block, axis, route)  6.02 us
    unnamed x115, local copies, waits for them, and re-layouts  5.81 us
  transfers between devices with their start and end apart: 3, of which 2 were waited for; matrix products, arithmetic and copies ran while one was open for 23% of the time, Pallas kernels for 0%

profile of v1, /device:TPU:1, one launch (start us, length us, event | category | flops | bytes accessed | tf_op | source)
XLA Modules:
  0.0 131.8 jit_solution(6127900512736252825)
XLA Ops:
  0.8 1.1 fusion.145
  1.9 2.2 %fusion.85 = (bf16[4,8,128,128]{3,1,2,0:T(8,128)(2,1)S(1)}, bf16[4,8,128,128]{3,1,2,0:T(8,128)(2,1)S(1)}) fusion(f32[16384]{0:T(1024)S(1)} %get-tuple-element.54, f32[16384]{0:T(1024)S(1)} %get-tuple-element.53, bf16[2,4,8,16384]{3,2,1,0:T(8,128)(2,1)} %param.6), kind=kLoop, calls=%fused_computation.137 | loop fusion | flops 5242880 | bytes 4325376
  4.1 0.6 copy_bitcast_fusion.1
  4.8 0.7 convolution_bitcast_fusion
  5.5 0.6 subtract_convert_fusion
  6.1 0.7 fusion.14
  6.9 0.8 copy.188
  7.7 1.6 %copy.90 = bf16[32,2,4,8,512]{4,3,1,2,0:T(8,128)(2,1)} copy(bf16[32,2,4,8,512]{4,3,2,1,0:T(8,128)(2,1)S(1)} %bitcast.565) | data formatting | bytes 4194304 | tf_op jit(solution)/shard_map/reshape | solution.py:130
  9.3 12.2 %all-to-all-start = ((bf16[32,2,4,8,512]{4,3,1,2,0:T(8,128)(2,1)}), bf16[32,2,4,8,512]{4,3,1,2,0:T(8,128)(2,1)S(1)}, u32[]{:S(2)}, u32[]{:S(2)}) async-start(bf16[32,2,4,8,512]{4,3,1,2,0:T(8,128)(2,1)} %copy.90), calls=%async_computation | async-start | bytes 4194304 | tf_op jit(solution)/shard_map/all_to_all | solution.py:131
  21.4 0.6 slice_reduce_fusion.39
  22.1 0.7 slice_reduce_fusion.30
  22.8 0.7 slice_reduce_fusion.31
  23.5 1.5 %fusion.120 = bf16[256,1,384]{2,0,1:T(8,128)(2,1)S(1)} fusion(), kind=kLoop, calls=%fused_computation.203 | loop fusion | flops 1081344 | bytes 196608 | tf_op jit(solution)/shard_map/convert.37
  25.0 2.3 %fusion.107 = bf16[384,1,384]{0,2,1:T(8,128)(2,1)S(1)} fusion(), kind=kLoop, calls=%fused_computation.184 | loop fusion | flops 1622016 | bytes 294912 | tf_op jit(solution)/shard_map/convert.29
  27.3 1.7 %negate_convert_fusion.1 = (bf16[256,1,384]{2,0,1:T(8,128)(2,1)S(1)}, bf16[256,1,384]{2,0,1:T(8,128)(2,1)S(1)}) fusion(), kind=kLoop, calls=%fused_computation.196 | loop fusion | flops 1376256 | bytes 393216 | tf_op jit(solution)/shard_map/convert.41
  29.1 2.6 %negate_convert_fusion = (bf16[384,1,384]{0,2,1:T(8,128)(2,1)S(1)}, bf16[384,1,384]{0,2,1:T(8,128)(2,1)S(1)}) fusion(), kind=kLoop, calls=%fused_computation.177 | loop fusion | flops 2064384 | bytes 589824 | tf_op jit(solution)/shard_map/convert.33
  31.7 1.0 maximum_bitcast_fusion.11
  32.8 0.6 iota_add_fusion.3
  33.5 36.4 %all-to-all-done = bf16[32,2,4,8,512]{4,3,1,2,0:T(8,128)(2,1)S(1)} async-done(((bf16[32,2,4,8,512]{4,3,1,2,0:T(8,128)(2,1)}), bf16[32,2,4,8,512]{4,3,1,2,0:T(8,128)(2,1)S(1)}, u32[]{:S(2)}, u32[]{:S(2)}) %all-to-all-start) | async-done | bytes 2097184 | tf_op jit(solution)/shard_map/all_to_all | solution.py:131
  70.1 4.7 %collective-permute-start = (bf16[16,2,4,8,512]{4,3,0,1,2:T(8,128)(2,1)S(1)}, bf16[16,2,4,8,512]{4,3,0,1,2:T(8,128)(2,1)S(1)}, u32[]{:S(2)}, u32[]{:S(2)}) collective-permute-start(bf16[16,2,4,8,512]{4,3,0,1,2:T(8,128)(2,1)S(1)} %copy.187), channel_id=1, source_target_pairs={{32,0},{64,32},{96,64},{128,96},{160,128},{192,160},{224,192},{33,... | collective-permute-start | bytes 3145736 | tf_op jit(solution)/shard_map/ppermute | solution.py:15
  74.9 1.9 %fusion.11 = f32[2,384,4,512,1,1]{3,1,5,4,2,0:T(8,128)S(1)} fusion(bf16[1,384,2,384]{1,3,2,0:T(8,128)(2,1)S(1)} %get-tuple-element.50, bf16[1,384,2,384]{1,3,2,0:T(8,128)(2,1)S(1)} %get-tuple-element.49, bf16[32,2,4,8,512]{4,3,1,2,0:T(8,128)(2,1)S(1)} %all-to-all-done), kind=kOutput, calls=%fused_computation.23 | convolution fusion | flops 1612185600 | bytes 9568256 | tf_op jit(solution)/shard_map/dot_general | solution.py:140
  76.8 11.8 %collective-permute-done = bf16[16,2,4,8,512]{4,3,0,1,2:T(8,128)(2,1)S(1)} collective-permute-done((bf16[16,2,4,8,512]{4,3,0,1,2:T(8,128)(2,1)S(1)}, bf16[16,2,4,8,512]{4,3,0,1,2:T(8,128)(2,1)S(1)}, u32[]{:S(2)}, u32[]{:S(2)}) %collective-permute-start) | collective-permute-done | bytes 1048608 | tf_op jit(solution)/shard_map/ppermute | solution.py:15
  88.6 2.1 %fusion = bf16[2,384,4,512]{3,1,2,0:T(8,128)(2,1)S(1)} fusion(f32[2,384,4,512,1,1]{3,1,5,4,2,0:T(8,128)S(1)} %fusion.11, bf16[16,2,4,8,512]{4,3,0,1,2:T(8,128)(2,1)S(1)} %collective-permute-done, bf16[1,384,2,384]{1,3,2,0:T(8,128)(2,1)} %copy-done.4, bf16[1,384,2,384]{1,3,2,0:T(8,128)(2,1)} %copy-done.5), kind=kOutput, calls=%fused_computation.2 | convolution fusion | flops 809238528 | bytes 11665408 | tf_op jit(solution)/shard_map/dot_general | solution.py:141
  90.8 1.0 slice.519
  91.8 1.4 %copy.119 = bf16[2,384,4,64]{1,3,2,0:T(8,128)(2,1)S(1)} copy(bf16[2,384,4,64]{3,1,2,0:T(8,128)(2,1)} %slice.519) | data formatting | bytes 786432 | tf_op jit(solution)/shard_map/slice | solution.py:143
  93.2 1.3 collective-permute-start.1
  94.5 1.8 %fusion.51 = f32[2,384,4,8,128]{1,4,2,0,3:T(8,128)S(1)} fusion(bf16[2,384,4,512]{3,1,2,0:T(8,128)(2,1)S(1)} %fusion, s32[8,128]{1,0:T(8,128)S(1)} %get-tuple-element.73), kind=kOutput, calls=%fused_computation.81 | convolution fusion | flops 1208156160 | bytes 14159872 | tf_op jit(solution)/shard_map/dot_general | solution.py:90
  96.4 1.8 %fusion.67 = f32[2,384,4,8,128]{1,4,2,0,3:T(8,128)S(1)} fusion(bf16[2,384,4,512]{3,1,2,0:T(8,128)(2,1)S(1)} %fusion, s32[8,128]{1,0:T(8,128)S(1)} %get-tuple-element.74), kind=kOutput, calls=%fused_computation.106 | convolution fusion | flops 1208156160 | bytes 14159872 | tf_op jit(solution)/shard_map/dot_general | solution.py:90
  98.3 6.4 %fusion.83 = f32[2,384,4,8,128]{1,4,3,2,0:T(8,128)} fusion(bf16[2,384,4,512]{3,1,2,0:T(8,128)(2,1)S(1)} %fusion, s32[8,128]{1,0:T(8,128)S(1)} %copy-done.53), kind=kOutput, calls=%fused_computation.131 | convolution fusion | flops 1208156160 | bytes 14159872 | tf_op jit(solution)/shard_map/dot_general | solution.py:90
  104.8 2.3 %fusion.37 = f32[2,384,4,128]{1,3,2,0:T(8,128)} fusion(f32[2,384,4,8,128]{1,4,2,0,3:T(8,128)S(1)} %fusion.51, f32[384]{0:T(512)S(1)} %copy-done.16, f32[384]{0:T(512)S(1)} %copy-done.18, f32[384]{0:T(512)S(1)} %copy-done.8, f32[384]{0:T(512)S(1)} %copy-done.9, f32[384]{0:T(512)S(1)} %copy-done.10, f32[384]{0:T(512)S(1)} %copy-done.12, f32[384]{0:T(512)S(1)} %copy-done.14, ...), kind=kLoop, calls=%fused_computation.59 | loop fusion | flops 5898240 | bytes 14168064 | tf_op jit(solution)/shard_map/add | solution.py:95
  107.0 2.3 %fusion.53 = f32[2,384,4,128]{1,3,2,0:T(8,128)} fusion(f32[2,384,4,8,128]{1,4,2,0,3:T(8,128)S(1)} %fusion.67, f32[384]{0:T(512)S(1)} %copy-done.16, f32[384]{0:T(512)S(1)} %copy-done.18, f32[384]{0:T(512)S(1)} %copy-done.8, f32[384]{0:T(512)S(1)} %copy-done.9, f32[384]{0:T(512)S(1)} %copy-done.10, f32[384]{0:T(512)S(1)} %copy-done.12, f32[384]{0:T(512)S(1)} %copy-done.14, ...), kind=kLoop, calls=%fused_computation.84 | loop fusion | flops 5898240 | bytes 14168064 | tf_op jit(solution)/shard_map/add | solution.py:95
  109.4 2.8 %copy-done = f32[2,384,4,8,128]{1,4,3,2,0:T(8,128)S(1)} copy-done((f32[2,384,4,8,128]{1,4,3,2,0:T(8,128)S(1)}, f32[2,384,4,8,128]{1,4,3,2,0:T(8,128)}, u32[]{:S(2)}) %copy-start) | copy-done | bytes 12582936
  112.2 2.3 %fusion.69 = f32[2,384,4,128]{1,3,2,0:T(8,128)} fusion(f32[2,384,4,8,128]{1,4,3,2,0:T(8,128)S(1)} %copy-done, f32[384]{0:T(512)S(1)} %copy-done.16, f32[384]{0:T(512)S(1)} %copy-done.18, f32[384]{0:T(512)S(1)} %copy-done.8, f32[384]{0:T(512)S(1)} %copy-done.9, f32[384]{0:T(512)S(1)} %copy-done.10, f32[384]{0:T(512)S(1)} %copy-done.12, ...), kind=kLoop, calls=%fused_computation.109 | loop fusion | flops 5898240 | bytes 14168064 | tf_op jit(solution)/shard_map/add | solution.py:95
  114.5 2.2 %copy.120 = bf16[2,384,4,64]{3,1,2,0:T(8,128)(2,1)} copy(bf16[2,384,4,64]{1,3,2,0:T(8,128)(2,1)} %collective-permute-done.1) | data formatting | bytes 786432 | tf_op jit(solution)/shard_map/ppermute | solution.py:15
  116.7 3.0 %fusion.33 = f32[2,384,4,8,128]{1,4,2,0,3:T(8,128)S(1)} fusion(bf16[2,384,4,64]{3,1,2,0:T(8,128)(2,1)} %copy.120, bf16[2,384,4,512]{3,1,2,0:T(8,128)(2,1)S(1)} %fusion, s32[8,128]{1,0:T(8,128)S(1)} %iota_add_fusion), kind=kOutput, calls=%fused_computation.55 | convolution fusion | flops 1210515456 | bytes 16125952 | tf_op jit(solution)/shard_map/dot_general | solution.py:90
  119.7 1.1 fusion.18
  121.1 0.5 copy-done.2
  121.6 0.5 copy-done.3
  122.1 0.7 pad_maximum_fusion
  122.9 0.4 subtract_convert_fusion.3
  124.1 0.4 subtract_convert_fusion.4
  124.6 0.4 add_convert_fusion.4
  125.3 0.4 subtract_convert_fusion.2
  125.8 0.4 add_convert_fusion.2
  126.4 0.4 subtract_convert_fusion.1
  126.9 0.4 add_convert_fusion.1
  127.9 0.7 copy-done.6
  128.7 3.1 %fusion.8 = bf16[2,4,256,512]{3,2,1,0:T(8,128)(2,1)} fusion(bf16[1,384,4,512]{1,3,2,0:T(8,128)(2,1)S(1)} %maximum_bitcast_fusion.8, bf16[1,384,4,512]{1,3,2,0:T(8,128)(2,1)S(1)} %maximum_bitcast_fusion.7, bf16[1,256,2,384]{3,1,2,0:T(8,128)(2,1)S(1)} %copy-done.7, bf16[1,256,2,384]{3,1,2,0:T(8,128)(2,1)S(1)} %copy-done.6), kind=kOutput, calls=%fused_computation.18 | convolution fusion | flops 1619525632 | bytes 6029312 | tf_op jit(solution)/shard_map/dot_general | solution.py:36
  (127 shorter events, 3.4 us)
Async XLA Ops:
  9.3 12.2 %copy-start.54 = (f32[8,384]{1,0:T(8,128)S(1)}, f32[8,384]{1,0:T(8,128)}, u32[]{:S(2)}) copy-start(f32[8,384]{1,0:T(8,128)} %param.9) | copy-start | bytes 36868
  9.3 12.8 %copy-start.55 = (f32[2,4,384]{2,1,0:T(4,128)S(1)}, f32[2,4,384]{2,1,0:T(4,128)}, u32[]{:S(2)}) copy-start(f32[2,4,384]{2,1,0:T(4,128)} %param.11) | copy-start | bytes 36868
  9.3 12.8 %copy-start.20 = (f32[2,4,4,384]{3,2,1,0:T(4,128)S(1)}, f32[2,4,4,384]{3,2,1,0:T(4,128)}, u32[]{:S(2)}) copy-start(f32[2,4,4,384]{3,2,1,0:T(4,128)} %param.10) | copy-start | bytes 147460
  9.3 60.6 %all-to-all-start = ((bf16[32,2,4,8,512]{4,3,1,2,0:T(8,128)(2,1)}), bf16[32,2,4,8,512]{4,3,1,2,0:T(8,128)(2,1)S(1)}, u32[]{:S(2)}, u32[]{:S(2)}) async-start(bf16[32,2,4,8,512]{4,3,1,2,0:T(8,128)(2,1)} %copy.90), calls=%async_computation | async-start | bytes 4194304 | tf_op jit(solution)/shard_map/all_to_all | solution.py:131
  31.7 1.1 copy-start.56
  32.8 42.1 %copy-start.4 = (bf16[1,384,2,384]{1,3,2,0:T(8,128)(2,1)}, bf16[1,384,2,384]{1,3,2,0:T(8,128)(2,1)S(1)}, u32[]{:S(2)}) copy-start(bf16[1,384,2,384]{1,3,2,0:T(8,128)(2,1)S(1)} %get-tuple-element.49) | copy-start | bytes 1769476
  32.8 42.1 %copy-start.5 = (bf16[1,384,2,384]{1,3,2,0:T(8,128)(2,1)}, bf16[1,384,2,384]{1,3,2,0:T(8,128)(2,1)S(1)}, u32[]{:S(2)}) copy-start(bf16[1,384,2,384]{1,3,2,0:T(8,128)(2,1)S(1)} %get-tuple-element.50) | copy-start | bytes 1769476
  70.1 18.5 %collective-permute-start = (bf16[16,2,4,8,512]{4,3,0,1,2:T(8,128)(2,1)S(1)}, bf16[16,2,4,8,512]{4,3,0,1,2:T(8,128)(2,1)S(1)}, u32[]{:S(2)}, u32[]{:S(2)}) collective-permute-start(bf16[16,2,4,8,512]{4,3,0,1,2:T(8,128)(2,1)S(1)} %copy.187), channel_id=1, source_target_pairs={{32,0},{64,32},{96,64},{128,96},{160,128},{192,160},{224,192},{33,... | collective-permute-start | bytes 3145736 | tf_op jit(solution)/shard_map/ppermute | solution.py:15
  93.2 21.3 %collective-permute-start.1 = (bf16[2,384,4,64]{1,3,2,0:T(8,128)(2,1)S(1)}, bf16[2,384,4,64]{1,3,2,0:T(8,128)(2,1)}, u32[]{:S(2)}, u32[]{:S(2)}) collective-permute-start(bf16[2,384,4,64]{1,3,2,0:T(8,128)(2,1)S(1)} %copy.119), channel_id=1, source_target_pairs={{1,0},{2,1},{3,2},{4,3},{5,4},{6,5},{7,6},{8,7},{9,8},{10,9},{11,1... | collective-permute-start | bytes 1179656 | tf_op jit(solution)/shard_map/ppermute | solution.py:15
  96.4 1.9 %copy-start.53 = (s32[8,128]{1,0:T(8,128)S(1)}, s32[8,128]{1,0:T(8,128)}, u32[]{:S(2)}) copy-start(s32[8,128]{1,0:T(8,128)} %iota_add_fusion.3) | copy-start | bytes 12292
  98.2 6.5 %copy-start.8 = (f32[384]{0:T(512)S(1)}, f32[384]{0:T(512)}, u32[]{:S(2)}) copy-start(f32[384]{0:T(512)} %get-tuple-element.38) | copy-start | bytes 4612
  98.2 6.5 %copy-start.9 = (f32[384]{0:T(512)S(1)}, f32[384]{0:T(512)}, u32[]{:S(2)}) copy-start(f32[384]{0:T(512)} %get-tuple-element.39) | copy-start | bytes 4612
  98.2 6.5 %copy-start.10 = (f32[384]{0:T(512)S(1)}, f32[384]{0:T(512)}, u32[]{:S(2)}) copy-start(f32[384]{0:T(512)} %get-tuple-element.40) | copy-start | bytes 4612
  98.3 6.5 %copy-start.12 = (f32[384]{0:T(512)S(1)}, f32[384]{0:T(512)}, u32[]{:S(2)}) copy-start(f32[384]{0:T(512)} %get-tuple-element.41) | copy-start | bytes 4612
  98.3 6.5 %copy-start.14 = (f32[384]{0:T(512)S(1)}, f32[384]{0:T(512)}, u32[]{:S(2)}) copy-start(f32[384]{0:T(512)} %get-tuple-element.42) | copy-start | bytes 4612
  98.3 6.5 %copy-start.16 = (f32[384]{0:T(512)S(1)}, f32[384]{0:T(512)}, u32[]{:S(2)}) copy-start(f32[384]{0:T(512)} %get-tuple-element.43) | copy-start | bytes 4612
  98.3 6.5 %copy-start.18 = (f32[384]{0:T(512)S(1)}, f32[384]{0:T(512)}, u32[]{:S(2)}) copy-start(f32[384]{0:T(512)} %get-tuple-element.44) | copy-start | bytes 4612
  107.0 5.1 %copy-start = (f32[2,384,4,8,128]{1,4,3,2,0:T(8,128)S(1)}, f32[2,384,4,8,128]{1,4,3,2,0:T(8,128)}, u32[]{:S(2)}) copy-start(f32[2,384,4,8,128]{1,4,3,2,0:T(8,128)} %fusion.83) | copy-start | bytes 37748740
  116.6 3.0 %copy-start.11 = (f32[384]{0:T(512)S(1)}, f32[384]{0:T(512)}, u32[]{:S(2)}) copy-start(f32[384]{0:T(512)} %get-tuple-element.40) | copy-start | bytes 4612
  116.6 3.0 %copy-start.13 = (f32[384]{0:T(512)S(1)}, f32[384]{0:T(512)}, u32[]{:S(2)}) copy-start(f32[384]{0:T(512)} %get-tuple-element.41) | copy-start | bytes 4612
  116.6 3.0 %copy-start.15 = (f32[384]{0:T(512)S(1)}, f32[384]{0:T(512)}, u32[]{:S(2)}) copy-start(f32[384]{0:T(512)} %get-tuple-element.42) | copy-start | bytes 4612
  116.6 3.0 %copy-start.17 = (f32[384]{0:T(512)S(1)}, f32[384]{0:T(512)}, u32[]{:S(2)}) copy-start(f32[384]{0:T(512)} %get-tuple-element.43) | copy-start | bytes 4612
  116.6 3.0 %copy-start.19 = (f32[384]{0:T(512)S(1)}, f32[384]{0:T(512)}, u32[]{:S(2)}) copy-start(f32[384]{0:T(512)} %get-tuple-element.44) | copy-start | bytes 4612
  119.7 1.4 %copy-start.1 = (f32[2,384,4,128]{1,3,2,0:T(8,128)S(1)}, f32[2,384,4,128]{1,3,2,0:T(8,128)}, u32[]{:S(2)}) copy-start(f32[2,384,4,128]{1,3,2,0:T(8,128)} %fusion.37) | copy-start | bytes 4718596
  119.7 1.9 %copy-start.2 = (f32[2,384,4,128]{1,3,2,0:T(8,128)S(1)}, f32[2,384,4,128]{1,3,2,0:T(8,128)}, u32[]{:S(2)}) copy-start(f32[2,384,4,128]{1,3,2,0:T(8,128)} %fusion.53) | copy-start | bytes 4718596
  119.7 2.3 %copy-start.3 = (f32[2,384,4,128]{1,3,2,0:T(8,128)S(1)}, f32[2,384,4,128]{1,3,2,0:T(8,128)}, u32[]{:S(2)}) copy-start(f32[2,384,4,128]{1,3,2,0:T(8,128)} %fusion.69) | copy-start | bytes 4718596
  122.0 0.7 copy-start.37
  122.0 0.7 copy-start.38
  122.0 0.8 copy-start.39
  122.1 0.8 copy-start.40
  122.1 0.8 copy-start.49
  122.1 0.8 copy-start.50
  122.1 0.8 copy-start.51
  122.1 0.8 copy-start.52
  123.3 0.7 copy-start.29
  123.3 0.7 copy-start.31
  123.3 0.7 copy-start.32
  123.3 0.7 copy-start.45
  123.4 0.7 copy-start.46
  123.4 0.7 copy-start.47
  123.4 0.7 copy-start.48
  124.5 0.7 copy-start.26
  124.6 0.7 copy-start.43
  124.6 0.7 copy-start.44
  125.7 0.7 copy-start.23
  125.7 0.7 copy-start.24
  127.6 1.0 copy-start.6
  127.6 1.1 copy-start.7
  (12 other events, 7.9 us)

commit v2 on v1

--- a/solution.py
+++ b/solution.py
@@ -4,6 +4,7 @@
 import jax.numpy as jnp
 from jax import lax
 from jax.sharding import PartitionSpec as P
+
 
 R1 = 128
 MARG = 64
@@ -38,41 +39,6 @@
     )
 
 
-def compress(echoes, range_phase):
-    cosine = jnp.cos(range_phase)
-    sine = jnp.sin(range_phase)
-    real_in = echoes[0].astype(jnp.float32)
-    imag_in = echoes[1].astype(jnp.float32)
-    spectrum = jnp.stack(
-        [real_in * cosine - imag_in * sine, real_in * sine + imag_in * cosine]
-    ).astype(jnp.bfloat16)
-    channels = spectrum.shape[1]
-    pulses = spectrum.shape[2]
-    range_bins = spectrum.shape[3]
-    second = range_bins // R1
-    spectrum = spectrum.reshape((2, channels, pulses, R1, second))
-    section = apply_table(complex_table(R1, R1, R1, 1.0, 1.0), spectrum, 0, 3)
-    twist_re, twist_im = phase_pair(R1, second, range_bins, 1.0, 1.0 / math.sqrt(range_bins))
-    twist_re = twist_re[:, None, None, :]
-    twist_im = twist_im[:, None, None, :]
-    partial_terms = jnp.stack(
-        [
-            section[0] * twist_re - section[1] * twist_im,
-            section[0] * twist_im + section[1] * twist_re,
-        ]
-    ).astype(jnp.bfloat16)
-    result = apply_table(
-        complex_table(second, second, second, 1.0, 1.0), partial_terms, 0, 4
-    ).astype(jnp.bfloat16)
-    return result.transpose(0, 3, 4, 1, 2).reshape((2, channels, pulses, range_bins))
-
-
-def doppler(window):
-    wide = window.shape[2]
-    forward = complex_table(wide, wide, wide, -1.0, 1.0 / math.sqrt(wide))
-    return apply_table(forward, window, 0, 2).astype(jnp.bfloat16)
-
-
 def migrate(extended, offsets, tap_weights, block):
     tile = min(128, block)
     taps = tap_weights.shape[0]
@@ -88,18 +54,20 @@
         ).astype(jnp.bfloat16)
         window_part = extended[:, :, :, first : first + tile + MARG]
         picked = lax.dot_general(
-            window_part, onehot, (((3,), (2,)), ((), ())), preferred_element_type=jnp.float32
+            window_part, onehot, (((3,), (2,)), ((), ())), preferred_element_type=jnp.bfloat16
         )
         total = jnp.zeros(picked.shape[:3] + (tile,), jnp.float32)
         for tap_index in range(taps):
-            total = total + picked[:, :, :, tap_index] * tap_weights[tap_index][None, :, None, None]
+            total = total + picked[:, :, :, tap_index].astype(jnp.float32) * tap_weights[tap_index][None, :, None, None]
         pieces.append(total)
     return jnp.concatenate(pieces, axis=3)
 
 
-def body(echoes, range_phase, offsets, tap_weights, channel_mix, azimuth_filter):
-    dev_count = lax.axis_size("dev")
-    parts, channels, pulses, range_bins = echoes.shape
+CHUNKS = 2
+
+
+def compress_block(echoes, range_phase, dev_count):
+    _, channels, pulses, range_bins = echoes.shape
     second = range_bins // R1
     per_block = second // dev_count
     block = range_bins // dev_count
@@ -127,22 +95,35 @@
     result = lax.dot_general(
         second_table, partial_terms, (((3, 4), (0, 4)), ((), ())), preferred_element_type=jnp.float32
     ).astype(jnp.bfloat16)
-    result = result.transpose(0, 2, 3, 4, 1, 5).reshape((dev_count, 2, channels, pulses, block))
-    turned = lax.all_to_all(result, "dev", 0, 0, tiled=True)
+    return result.transpose(0, 2, 3, 4, 1, 5).reshape((dev_count, 2, channels, pulses, block))
+
+
+def body(echoes, range_phase, offsets, tap_weights, channel_mix, azimuth_filter):
+    dev_count = lax.axis_size("dev")
+    _, channels, pulses, range_bins = echoes.shape
+    block = range_bins // dev_count
     group_pulses = dev_count * pulses
     wide = group_pulses + group_pulses // 2
-    following = shifted(turned[: dev_count // 2], "blk", -1)
     forward = complex_table(wide, wide, wide, -1.0, 1.0 / math.sqrt(wide))
     own_table = forward[:, :, :, :group_pulses].reshape((2, wide, 2, dev_count, pulses))
     next_table = forward[:, :, :, group_pulses:].reshape((2, wide, 2, dev_count // 2, pulses))
     dims = (((2, 3, 4), (1, 0, 3)), ((), ()))
-    spectra = (
-        lax.dot_general(own_table, turned, dims, preferred_element_type=jnp.float32)
-        + lax.dot_general(next_table, following, dims, preferred_element_type=jnp.float32)
-    ).astype(jnp.bfloat16)
-    border = shifted(spectra[:, :, :, :MARG], "dev", -1)
-    extended = jnp.concatenate([spectra, border], axis=3)
-    moved = migrate(extended, offsets, tap_weights, block)
+    step = channels // CHUNKS
+    pieces = []
+    for chunk in range(CHUNKS):
+        result = compress_block(
+            echoes[:, chunk * step : (chunk + 1) * step], range_phase, dev_count
+        )
+        turned = lax.all_to_all(result, "dev", 0, 0, tiled=True)
+        following = shifted(turned[: dev_count // 2], "blk", -1)
+        spectra = (
+            lax.dot_general(own_table, turned, dims, preferred_element_type=jnp.float32)
+            + lax.dot_general(next_table, following, dims, preferred_element_type=jnp.float32)
+        ).astype(jnp.bfloat16)
+        border = shifted(spectra[:, :, :, :MARG], "dev", -1)
+        extended = jnp.concatenate([spectra, border], axis=3)
+        pieces.append(migrate(extended, offsets, tap_weights, block))
+    moved = jnp.concatenate(pieces, axis=2)
     mix_real = (
         azimuth_filter[0][:, None, :] * channel_mix[0]
         - azimuth_filter[1][:, None, :] * channel_mix[1]

time: 134 us -> 130 us (0.970)
  the two profiles are of different devices: /device:TPU:1 before, /device:TPU:27 now
where the time goes in v2:
time: 130 us; the launch traced here: 129 us
  waiting for transfers between devices  51.2 us (39%)
  starting transfers between devices  31.1 us (24%)
  other arithmetic  22.2 us (17%)
  matrix products  17.7 us (14%)
  local copies, waits for them, and re-layouts  6.75 us (5%)
    all_to_all x2, waiting for transfers between devices, body(): turned = lax.all_to_all(result, 'dev', 0, 0, tiled=True)  36.1 us
    all_to_all x2, starting transfers between devices, body(): turned = lax.all_to_all(result, 'dev', 0, 0, tiled=True)  16.4 us
    ppermute x4, waiting for transfers between devices, shifted(): return lax.ppermute(block, axis, route)  15.1 us
    ppermute x4, starting transfers between devices, shifted(): return lax.ppermute(block, axis, route)  14.7 us
    another operation x15, other arithmetic  12.8 us
    dot_general x8, matrix products, migrate(): lax.dot_general(window_part, onehot, (((3,), (2,)), ((), ())), preferred_...  8.27 us
    add x8, other arithmetic, migrate(): total + picked[:, :, :, tap_index].astype(jnp.float32) * tap_weights[tap_...  4.83 us
    dot_general x3, matrix products, apply_table(): lax.dot_general(table, data, (((2, 3), (part_dim, index_dim)), ((), ())),...  4.02 us
  transfers between devices with their start and end apart: 6, of which 5 were waited for; matrix products, arithmetic and copies ran while one was open for 17% of the time, Pallas kernels for 0%

profile of v2, /device:TPU:27, one launch (start us, length us, event | category | flops | bytes accessed | tf_op | source)
XLA Modules:
  0.0 129.4 jit_solution(9576960977741618280)
XLA Ops:
  0.8 1.1 fusion.175
  1.9 2.2 %fusion.122 = (bf16[2,8,128,128]{3,1,2,0:T(8,128)(2,1)S(1)}, bf16[2,8,128,128]{3,1,2,0:T(8,128)(2,1)S(1)}, bf16[2,8,128,128]{3,1,2,0:T(8,128)(2,1)S(1)}, bf16[2,8,128,128]{3,1,2,0:T(8,128)(2,1)S(1)}) fusion(f32[16384]{0:T(1024)S(1)} %get-tuple-element.60, f32[16384]{0:T(1024)S(1)} %get-tuple-element.59, bf16[2,4,8,16384]{3,2,1,0:T(8,128)(2,1)} %param.6), kind=kLoop, calls=%fused_computation.244 | loop fusion | flops 5242880 | bytes 4325376
  5.5 0.6 subtract_convert_fusion
  6.1 0.5 fusion.7
  7.0 1.1 copy.211
  8.2 10.9 %all-to-all-start.1 = ((bf16[32,2,2,8,512]{4,3,1,2,0:T(8,128)(2,1)}), bf16[32,2,2,8,512]{4,3,1,2,0:T(8,128)(2,1)S(1)}, u32[]{:S(2)}, u32[]{:S(2)}) async-start(bf16[32,2,2,8,512]{4,3,1,2,0:T(8,128)(2,1)} %copy.211), calls=%async_computation.1 | async-start | bytes 2097152 | tf_op jit(solution)/shard_map/all_to_all | solution.py:117
  19.1 0.5 fusion.6
  20.0 1.1 copy.170
  21.1 25.1 %all-to-all-done.1 = bf16[32,2,2,8,512]{4,3,1,2,0:T(8,128)(2,1)S(1)} async-done(((bf16[32,2,2,8,512]{4,3,1,2,0:T(8,128)(2,1)}), bf16[32,2,2,8,512]{4,3,1,2,0:T(8,128)(2,1)S(1)}, u32[]{:S(2)}, u32[]{:S(2)}) %all-to-all-start.1) | async-done | bytes 1048608 | tf_op jit(solution)/shard_map/all_to_all | solution.py:117
  46.2 5.5 %all-to-all-start = ((bf16[32,2,2,8,512]{4,3,1,2,0:T(8,128)(2,1)}), bf16[32,2,2,8,512]{4,3,1,2,0:T(8,128)(2,1)S(1)}, u32[]{:S(2)}, u32[]{:S(2)}) async-start(bf16[32,2,2,8,512]{4,3,1,2,0:T(8,128)(2,1)} %copy.170), calls=%async_computation | async-start | bytes 2097152 | tf_op jit(solution)/shard_map/all_to_all | solution.py:117
  51.9 1.5 %fusion.141 = bf16[256,1,384]{2,0,1:T(8,128)(2,1)S(1)} fusion(), kind=kLoop, calls=%fused_computation.338 | loop fusion | flops 1081344 | bytes 196608 | tf_op jit(solution)/shard_map/convert.107
  53.5 2.3 %fusion.120 = bf16[384,1,384]{0,2,1:T(8,128)(2,1)S(1)} fusion(), kind=kLoop, calls=%fused_computation.242 | loop fusion | flops 1622016 | bytes 294912 | tf_op jit(solution)/shard_map/convert.99
  55.8 1.7 %negate_convert_fusion.1 = (bf16[256,1,384]{2,0,1:T(8,128)(2,1)S(1)}, bf16[256,1,384]{2,0,1:T(8,128)(2,1)S(1)}) fusion(), kind=kLoop, calls=%fused_computation.331 | loop fusion | flops 1376256 | bytes 393216 | tf_op jit(solution)/shard_map/convert.111
  57.5 2.6 %negate_convert_fusion = (bf16[384,1,384]{0,2,1:T(8,128)(2,1)S(1)}, bf16[384,1,384]{0,2,1:T(8,128)(2,1)S(1)}) fusion(), kind=kLoop, calls=%fused_computation.235 | loop fusion | flops 2064384 | bytes 589824 | tf_op jit(solution)/shard_map/convert.103
  60.1 1.0 maximum_bitcast_fusion.14
  61.3 0.8 copy.342
  62.2 4.2 %collective-permute-start.2 = (bf16[16,2,2,8,512]{4,3,0,1,2:T(8,128)(2,1)}, bf16[16,2,2,8,512]{4,3,0,1,2:T(8,128)(2,1)}, u32[]{:S(2)}, u32[]{:S(2)}) collective-permute-start(bf16[16,2,2,8,512]{4,3,0,1,2:T(8,128)(2,1)} %copy.342), channel_id=1, source_target_pairs={{32,0},{64,32},{96,64},{128,96},{160,128},{192,160},{224,192},{33,... | collective-permute-start | bytes 1572872 | tf_op jit(solution)/shard_map/ppermute | solution.py:16
  66.4 11.0 %all-to-all-done = bf16[32,2,2,8,512]{4,3,1,2,0:T(8,128)(2,1)S(1)} async-done(((bf16[32,2,2,8,512]{4,3,1,2,0:T(8,128)(2,1)}), bf16[32,2,2,8,512]{4,3,1,2,0:T(8,128)(2,1)S(1)}, u32[]{:S(2)}, u32[]{:S(2)}) %all-to-all-start) | async-done | bytes 1048608 | tf_op jit(solution)/shard_map/all_to_all | solution.py:117
  77.5 5.6 %collective-permute-start = (bf16[16,2,2,8,512]{4,3,0,1,2:T(8,128)(2,1)S(1)}, bf16[16,2,2,8,512]{4,3,0,1,2:T(8,128)(2,1)S(1)}, u32[]{:S(2)}, u32[]{:S(2)}) collective-permute-start(bf16[16,2,2,8,512]{4,3,0,1,2:T(8,128)(2,1)S(1)} %copy.341), channel_id=1, source_target_pairs={{32,0},{64,32},{96,64},{128,96},{160,128},{192,160},{224,192},{33,... | collective-permute-start | bytes 1572872 | tf_op jit(solution)/shard_map/ppermute | solution.py:16
  83.1 1.0 fusion.20
  84.2 1.0 fusion.23
  85.2 1.7 %fusion.3 = bf16[2,384,2,512]{3,1,2,0:T(8,128)(2,1)S(1)} fusion(f32[2,384,2,512,1,1]{3,1,5,4,2,0:T(8,128)S(1)} %fusion.20, bf16[16,2,2,8,512]{4,3,0,1,2:T(8,128)(2,1)} %collective-permute-done.2, bf16[1,384,2,384]{1,3,2,0:T(8,128)(2,1)S(1)} %get-tuple-element.53, bf16[1,384,2,384]{1,3,2,0:T(8,128)(2,1)S(1)} %get-tuple-element.54), kind=kOutput, calls=%fused_computation.8 | convolution fusion | flops 405012480 | bytes 6422528 | tf_op jit(solution)/shard_map/dot_general | solution.py:121
  87.0 1.0 fusion.32
  88.1 2.8 %collective-permute-done = bf16[16,2,2,8,512]{4,3,0,1,2:T(8,128)(2,1)S(1)} collective-permute-done((bf16[16,2,2,8,512]{4,3,0,1,2:T(8,128)(2,1)S(1)}, bf16[16,2,2,8,512]{4,3,0,1,2:T(8,128)(2,1)S(1)}, u32[]{:S(2)}, u32[]{:S(2)}) %collective-permute-start) | collective-permute-done | bytes 524320 | tf_op jit(solution)/shard_map/ppermute | solution.py:16
  90.9 0.7 fusion.4
  91.6 1.0 fusion.39
  92.7 1.0 fusion.33
  93.7 1.0 fusion.40
  94.7 1.0 fusion.34
  95.8 1.0 fusion.41
  96.8 2.5 %collective-permute-start.3 = (bf16[2,384,2,64]{3,1,2,0:T(8,128)(2,1)S(1)}, bf16[2,384,2,64]{3,1,2,0:T(8,128)(2,1)S(1)}, u32[]{:S(2)}, u32[]{:S(2)}) collective-permute-start(bf16[2,384,2,64]{3,1,2,0:T(8,128)(2,1)S(1)} %slice.778), channel_id=1, source_target_pairs={{1,0},{2,1},{3,2},{4,3},{5,4},{6,5},{7,6},{8,7},{9,8},{10,9},{11,1... | collective-permute-start | bytes 589832 | tf_op jit(solution)/shard_map/ppermute | solution.py:16
  99.3 0.6 fusion.53
  99.9 0.6 fusion.60
  100.5 0.6 fusion.67
  101.1 2.4 %collective-permute-start.1 = (bf16[2,384,2,64]{3,1,2,0:T(8,128)(2,1)S(1)}, bf16[2,384,2,64]{3,1,2,0:T(8,128)(2,1)S(1)}, u32[]{:S(2)}, u32[]{:S(2)}) collective-permute-start(bf16[2,384,2,64]{3,1,2,0:T(8,128)(2,1)S(1)} %slice.731), channel_id=1, source_target_pairs={{1,0},{2,1},{3,2},{4,3},{5,4},{6,5},{7,6},{8,7},{9,8},{10,9},{11,1... | collective-permute-start | bytes 589832 | tf_op jit(solution)/shard_map/ppermute | solution.py:16
  103.6 0.6 fusion.81
  104.2 0.6 fusion.88
  104.8 0.6 fusion.95
  105.4 6.6 %collective-permute-done.3 = bf16[2,384,2,64]{3,1,2,0:T(8,128)(2,1)S(1)} collective-permute-done((bf16[2,384,2,64]{3,1,2,0:T(8,128)(2,1)S(1)}, bf16[2,384,2,64]{3,1,2,0:T(8,128)(2,1)S(1)}, u32[]{:S(2)}, u32[]{:S(2)}) %collective-permute-start.3) | collective-permute-done | bytes 196640 | tf_op jit(solution)/shard_map/ppermute | solution.py:16
  112.0 1.0 fusion.29
  113.0 0.6 fusion.46
  113.6 5.7 %collective-permute-done.1 = bf16[2,384,2,64]{3,1,2,0:T(8,128)(2,1)S(1)} collective-permute-done((bf16[2,384,2,64]{3,1,2,0:T(8,128)(2,1)S(1)}, bf16[2,384,2,64]{3,1,2,0:T(8,128)(2,1)S(1)}, u32[]{:S(2)}, u32[]{:S(2)}) %collective-permute-start.1) | collective-permute-done | bytes 196640 | tf_op jit(solution)/shard_map/ppermute | solution.py:16
  119.3 1.0 fusion.36
  120.4 0.6 fusion.74
  122.3 0.4 subtract_convert_fusion.4
  123.2 0.4 subtract_convert_fusion.3
  125.4 0.7 copy-done
  126.3 3.1 %fusion.5 = bf16[2,4,256,512]{3,2,1,0:T(8,128)(2,1)} fusion(bf16[1,384,4,512]{1,3,2,0:T(8,128)(2,1)S(1)} %maximum_bitcast_fusion.5, bf16[1,384,4,512]{1,3,2,0:T(8,128)(2,1)S(1)} %maximum_bitcast_fusion.4, bf16[1,256,2,384]{3,1,2,0:T(8,128)(2,1)S(1)} %copy-done.1, bf16[1,256,2,384]{3,1,2,0:T(8,128)(2,1)S(1)} %copy-done), kind=kOutput, calls=%fused_computation.11 | convolution fusion | flops 1619525632 | bytes 6029312 | tf_op jit(solution)/shard_map/dot_general | solution.py:37
  (48 shorter events, 7.3 us)
Async XLA Ops:
  8.2 38.0 %all-to-all-start.1 = ((bf16[32,2,2,8,512]{4,3,1,2,0:T(8,128)(2,1)}), bf16[32,2,2,8,512]{4,3,1,2,0:T(8,128)(2,1)S(1)}, u32[]{:S(2)}, u32[]{:S(2)}) async-start(bf16[32,2,2,8,512]{4,3,1,2,0:T(8,128)(2,1)} %copy.211), calls=%async_computation.1 | async-start | bytes 2097152 | tf_op jit(solution)/shard_map/all_to_all | solution.py:117
  19.5 1.6 %copy-start.4 = (f32[2,4,384]{2,1,0:T(4,128)S(1)}, f32[2,4,384]{2,1,0:T(4,128)}, u32[]{:S(2)}) copy-start(f32[2,4,384]{2,1,0:T(4,128)} %param.11) | copy-start | bytes 36868
  20.0 31.7 %copy-start.2 = (f32[2,4,4,384]{3,2,1,0:T(4,128)S(1)}, f32[2,4,4,384]{3,2,1,0:T(4,128)}, u32[]{:S(2)}) copy-start(f32[2,4,4,384]{3,2,1,0:T(4,128)} %param.10) | copy-start | bytes 147460
  20.0 31.7 %copy-start.3 = (f32[8,384]{1,0:T(8,128)S(1)}, f32[8,384]{1,0:T(8,128)}, u32[]{:S(2)}) copy-start(f32[8,384]{1,0:T(8,128)} %param.9) | copy-start | bytes 36868
  46.2 31.2 %all-to-all-start = ((bf16[32,2,2,8,512]{4,3,1,2,0:T(8,128)(2,1)}), bf16[32,2,2,8,512]{4,3,1,2,0:T(8,128)(2,1)S(1)}, u32[]{:S(2)}, u32[]{:S(2)}) async-start(bf16[32,2,2,8,512]{4,3,1,2,0:T(8,128)(2,1)} %copy.170), calls=%async_computation | async-start | bytes 2097152 | tf_op jit(solution)/shard_map/all_to_all | solution.py:117
  57.5 3.7 %copy-start.5 = (s32[512]{0:T(512)S(1)}, s32[512]{0:T(512)}, u32[]{:S(2)}) copy-start(s32[512]{0:T(512)} %param.8) | copy-start | bytes 6148
  62.2 23.1 %collective-permute-start.2 = (bf16[16,2,2,8,512]{4,3,0,1,2:T(8,128)(2,1)}, bf16[16,2,2,8,512]{4,3,0,1,2:T(8,128)(2,1)}, u32[]{:S(2)}, u32[]{:S(2)}) collective-permute-start(bf16[16,2,2,8,512]{4,3,0,1,2:T(8,128)(2,1)} %copy.342), channel_id=1, source_target_pairs={{32,0},{64,32},{96,64},{128,96},{160,128},{192,160},{224,192},{33,... | collective-permute-start | bytes 1572872 | tf_op jit(solution)/shard_map/ppermute | solution.py:16
  77.5 13.4 %collective-permute-start = (bf16[16,2,2,8,512]{4,3,0,1,2:T(8,128)(2,1)S(1)}, bf16[16,2,2,8,512]{4,3,0,1,2:T(8,128)(2,1)S(1)}, u32[]{:S(2)}, u32[]{:S(2)}) collective-permute-start(bf16[16,2,2,8,512]{4,3,0,1,2:T(8,128)(2,1)S(1)} %copy.341), channel_id=1, source_target_pairs={{32,0},{64,32},{96,64},{128,96},{160,128},{192,160},{224,192},{33,... | collective-permute-start | bytes 1572872 | tf_op jit(solution)/shard_map/ppermute | solution.py:16
  96.8 15.1 %collective-permute-start.3 = (bf16[2,384,2,64]{3,1,2,0:T(8,128)(2,1)S(1)}, bf16[2,384,2,64]{3,1,2,0:T(8,128)(2,1)S(1)}, u32[]{:S(2)}, u32[]{:S(2)}) collective-permute-start(bf16[2,384,2,64]{3,1,2,0:T(8,128)(2,1)S(1)} %slice.778), channel_id=1, source_target_pairs={{1,0},{2,1},{3,2},{4,3},{5,4},{6,5},{7,6},{8,7},{9,8},{10,9},{11,1... | collective-permute-start | bytes 589832 | tf_op jit(solution)/shard_map/ppermute | solution.py:16
  101.1 18.2 %collective-permute-start.1 = (bf16[2,384,2,64]{3,1,2,0:T(8,128)(2,1)S(1)}, bf16[2,384,2,64]{3,1,2,0:T(8,128)(2,1)S(1)}, u32[]{:S(2)}, u32[]{:S(2)}) collective-permute-start(bf16[2,384,2,64]{3,1,2,0:T(8,128)(2,1)S(1)} %slice.731), channel_id=1, source_target_pairs={{1,0},{2,1},{3,2},{4,3},{5,4},{6,5},{7,6},{8,7},{9,8},{10,9},{11,1... | collective-permute-start | bytes 589832 | tf_op jit(solution)/shard_map/ppermute | solution.py:16
  125.2 1.0 copy-start
  125.2 1.1 copy-start.1

commit v3 on v2

--- a/solution.py
+++ b/solution.py
@@ -63,7 +63,7 @@
     return jnp.concatenate(pieces, axis=3)
 
 
-CHUNKS = 2
+SPLIT = (3, 1)
 
 
 def compress_block(echoes, range_phase, dev_count):
@@ -100,7 +100,7 @@
 
 def body(echoes, range_phase, offsets, tap_weights, channel_mix, azimuth_filter):
     dev_count = lax.axis_size("dev")
-    _, channels, pulses, range_bins = echoes.shape
+    _, _, pulses, range_bins = echoes.shape
     block = range_bins // dev_count
     group_pulses = dev_count * pulses
     wide = group_pulses + group_pulses // 2
@@ -108,12 +108,11 @@
     own_table = forward[:, :, :, :group_pulses].reshape((2, wide, 2, dev_count, pulses))
     next_table = forward[:, :, :, group_pulses:].reshape((2, wide, 2, dev_count // 2, pulses))
     dims = (((2, 3, 4), (1, 0, 3)), ((), ()))
-    step = channels // CHUNKS
     pieces = []
-    for chunk in range(CHUNKS):
-        result = compress_block(
-            echoes[:, chunk * step : (chunk + 1) * step], range_phase, dev_count
-        )
+    first = 0
+    for width in SPLIT:
+        result = compress_block(echoes[:, first : first + width], range_phase, dev_count)
+        first += width
         turned = lax.all_to_all(result, "dev", 0, 0, tiled=True)
         following = shifted(turned[: dev_count // 2], "blk", -1)
         spectra = (
@@ -132,25 +131,16 @@
         azimuth_filter[0][:, None, :] * channel_mix[1]
         + azimuth_filter[1][:, None, :] * channel_mix[0]
     )
-    rows_real = []
-    rows_imag = []
-    for channel in range(channels):
-        sum_real = jnp.zeros((wide, block), jnp.float32)
-        sum_imag = jnp.zeros((wide, block), jnp.float32)
-        for other_chan in range(channels):
-            coef_real = mix_real[channel, other_chan][:, None]
-            coef_imag = mix_imag[channel, other_chan][:, None]
-            sum_real = (
-                sum_real + coef_real * moved[0, :, other_chan] - coef_imag * moved[1, :, other_chan]
-            )
-            sum_imag = (
-                sum_imag + coef_real * moved[1, :, other_chan] + coef_imag * moved[0, :, other_chan]
-            )
-        rows_real.append(sum_real)
-        rows_imag.append(sum_imag)
-    focused = jnp.stack([jnp.stack(rows_real, axis=1), jnp.stack(rows_imag, axis=1)]).astype(
-        jnp.bfloat16
-    )
+    mix_real = mix_real.transpose(2, 0, 1)[:, :, :, None]
+    mix_imag = mix_imag.transpose(2, 0, 1)[:, :, :, None]
+    moved_real = moved[0][:, None]
+    moved_imag = moved[1][:, None]
+    focused = jnp.stack(
+        [
+            (mix_real * moved_real - mix_imag * moved_imag).sum(axis=2),
+            (mix_real * moved_imag + mix_imag * moved_real).sum(axis=2),
+        ]
+    ).astype(jnp.bfloat16)
     backward = complex_table(group_pulses, wide, wide, 1.0, 1.0 / math.sqrt(wide))
     image = apply_table(backward, focused, 0, 1).astype(jnp.bfloat16)
     return image.transpose(0, 2, 1, 3)

time: 130 us -> 150 us (1.15)
  the two profiles are of different devices: /device:TPU:27 before, /device:TPU:125 now
where the time goes in v3:
time: 150 us
  waiting for transfers between devices  38.5 us (26%)
  other arithmetic  33.1 us (22%)
  starting transfers between devices  31.6 us (21%)
  matrix products  26.8 us (18%)
  local copies, waits for them, and re-layouts  19.1 us (13%)
    ppermute x4, waiting for transfers between devices, shifted(): return lax.ppermute(block, axis, route)  38.5 us
    all_to_all x2, starting transfers between devices, body(): turned = lax.all_to_all(result, 'dev', 0, 0, tiled=True)  18.8 us
    dot_general x8, matrix products, migrate(): lax.dot_general(window_part, onehot, (((3,), (2,)), ((), ())), preferred_...  17.4 us
    ppermute x4, starting transfers between devices, shifted(): return lax.ppermute(block, axis, route)  12.8 us
    add x8, other arithmetic, migrate(): total + picked[:, :, :, tap_index].astype(jnp.float32) * tap_weights[tap_...  12.1 us
    another operation x7, other arithmetic  9.16 us
    reduce_sum x1, other arithmetic, body(): (mix_real * moved_real - mix_imag * moved_imag).sum(axis=2)  6.6 us
    mul x2, local copies, waits for them, and re-layouts, body(): mix_real * moved_real - mix_imag * moved_imag  5.46 us
  transfers between devices with their start and end apart: 6, of which 4 were waited for; matrix products, arithmetic and copies ran while one was open for 22% of the time, Pallas kernels for 0%

profile of v3, /device:TPU:125, one launch (start us, length us, event | category | flops | bytes accessed | tf_op | source)
XLA Modules:
  0.0 149.8 jit_solution(12427681811150710330)
XLA Ops:
  0.8 1.1 fusion.190
  2.0 1.2 fusion.157
  4.1 1.0 copy.499
  5.1 9.6 %all-to-all-start.1 = ((bf16[32,2,1,8,512]{4,3,1,2,0:T(8,128)(2,1)}), bf16[32,2,1,8,512]{4,3,1,2,0:T(8,128)(2,1)S(1)}, u32[]{:S(2)}, u32[]{:S(2)}) async-start(bf16[32,2,1,8,512]{4,3,1,2,0:T(8,128)(2,1)} %bitcast.871), calls=%async_computation.1 | async-start | bytes 1048576 | tf_op jit(solution)/shard_map/all_to_all | solution.py:116
  15.2 2.6 %negate_convert_fusion = (bf16[384,1,384]{0,2,1:T(8,128)(2,1)S(1)}, bf16[384,1,384]{0,2,1:T(8,128)(2,1)S(1)}) fusion(), kind=kLoop, calls=%fused_computation.197 | loop fusion | flops 2064384 | bytes 589824 | tf_op jit(solution)/shard_map/convert.97
  17.8 2.3 %fusion.86 = bf16[384,1,384]{0,2,1:T(8,128)(2,1)S(1)} fusion(), kind=kLoop, calls=%fused_computation.204 | loop fusion | flops 1622016 | bytes 294912 | tf_op jit(solution)/shard_map/convert.93
  20.1 1.7 %negate_convert_fusion.1 = (bf16[256,1,384]{2,0,1:T(8,128)(2,1)S(1)}, bf16[256,1,384]{2,0,1:T(8,128)(2,1)S(1)}) fusion(), kind=kLoop, calls=%fused_computation.299 | loop fusion | flops 1376256 | bytes 393216 | tf_op jit(solution)/shard_map/convert.105
  21.9 1.5 %fusion.153 = bf16[256,1,384]{2,0,1:T(8,128)(2,1)S(1)} fusion(), kind=kLoop, calls=%fused_computation.306 | loop fusion | flops 1081344 | bytes 196608 | tf_op jit(solution)/shard_map/convert.101
  25.7 1.0 maximum_bitcast_fusion.10
  26.7 1.0 maximum_bitcast_fusion.14
  28.3 1.3 copy.303
  29.8 0.6 fusion.178
  30.4 9.2 %all-to-all-start = ((bf16[32,2,3,8,512]{4,3,1,2,0:T(8,128)(2,1)}), bf16[32,2,3,8,512]{4,3,1,2,0:T(8,128)(2,1)S(1)}, u32[]{:S(2)}, u32[]{:S(2)}) async-start(bf16[32,2,3,8,512]{4,3,1,2,0:T(8,128)(2,1)} %copy.303), calls=%async_computation | async-start | bytes 3145728 | tf_op jit(solution)/shard_map/all_to_all | solution.py:116
  39.7 3.9 %collective-permute-start.2 = (bf16[16,2,1,8,512]{4,3,0,1,2:T(8,128)(2,1)S(1)}, bf16[16,2,1,8,512]{4,3,0,1,2:T(8,128)(2,1)S(1)}, u32[]{:S(2)}, u32[]{:S(2)}) collective-permute-start(bf16[16,2,1,8,512]{4,3,0,1,2:T(8,128)(2,1)S(1)} %copy.496), channel_id=1, source_target_pairs={{32,0},{64,32},{96,64},{128,96},{160,128},{192,160},{224,192},{33,... | collective-permute-start | bytes 786440 | tf_op jit(solution)/shard_map/ppermute | solution.py:16
  43.6 1.7 %fusion.63 = f32[2,384,512,1,1]{2,1,4,3,0:T(8,128)S(1)} fusion(bf16[32,2,1,8,512]{4,3,1,2,0:T(8,128)(2,1)S(1)} %all-to-all-done.1, bf16[1,384,2,384]{1,3,2,0:T(8,128)(2,1)} %get-tuple-element.26, bf16[1,384,2,384]{1,3,2,0:T(8,128)(2,1)S(1)} %get-tuple-element.25), kind=kOutput, calls=%fused_computation.130 | convolution fusion | flops 403046400 | bytes 3276800 | tf_op jit(solution)/shard_map/dot_general | solution.py:119
  45.3 3.3 %collective-permute-done.2 = bf16[16,2,1,8,512]{4,3,0,1,2:T(8,128)(2,1)S(1)} collective-permute-done((bf16[16,2,1,8,512]{4,3,0,1,2:T(8,128)(2,1)S(1)}, bf16[16,2,1,8,512]{4,3,0,1,2:T(8,128)(2,1)S(1)}, u32[]{:S(2)}, u32[]{:S(2)}) %collective-permute-start.2) | collective-permute-done | bytes 262176 | tf_op jit(solution)/shard_map/ppermute | solution.py:16
  49.0 2.5 %collective-permute-start.3 = (bf16[2,384,1,64]{3,1,0,2:T(8,128)(2,1)S(1)}, bf16[2,384,1,64]{3,1,0,2:T(8,128)(2,1)S(1)}, u32[]{:S(2)}, u32[]{:S(2)}) collective-permute-start(bf16[2,384,1,64]{3,1,0,2:T(8,128)(2,1)S(1)} %slice.563), channel_id=1, source_target_pairs={{1,0},{2,1},{3,2},{4,3},{5,4},{6,5},{7,6},{8,7},{9,8},{10,9},{11,1... | collective-permute-start | bytes 294920 | tf_op jit(solution)/shard_map/ppermute | solution.py:16
  51.5 0.8 convolution_bitcast_fusion.3
  52.3 0.8 convolution_bitcast_fusion.2
  53.1 0.8 convolution_bitcast_fusion.4
  53.9 1.0 fusion.112
  55.0 1.0 fusion.133
  56.0 1.1 fusion.104
  57.1 22.6 %collective-permute-done.3 = bf16[2,384,1,64]{3,1,0,2:T(8,128)(2,1)S(1)} collective-permute-done((bf16[2,384,1,64]{3,1,0,2:T(8,128)(2,1)S(1)}, bf16[2,384,1,64]{3,1,0,2:T(8,128)(2,1)S(1)}, u32[]{:S(2)}, u32[]{:S(2)}) %collective-permute-start.3) | collective-permute-done | bytes 98336 | tf_op jit(solution)/shard_map/ppermute | solution.py:16
  79.7 0.8 convolution_bitcast_fusion.1
  80.6 1.1 fusion.126
  81.8 4.0 %collective-permute-start = (bf16[16,2,3,8,512]{4,3,0,1,2:T(8,128)(2,1)S(1)}, bf16[16,2,3,8,512]{4,3,0,1,2:T(8,128)(2,1)S(1)}, u32[]{:S(2)}, u32[]{:S(2)}) collective-permute-start(bf16[16,2,3,8,512]{4,3,0,1,2:T(8,128)(2,1)S(1)} %copy.497), channel_id=1, source_target_pairs={{32,0},{64,32},{96,64},{128,96},{160,128},{192,160},{224,192},{33,... | collective-permute-start | bytes 2359304 | tf_op jit(solution)/shard_map/ppermute | solution.py:16
  85.8 1.5 fusion.12
  87.3 9.0 %collective-permute-done = bf16[16,2,3,8,512]{4,3,0,1,2:T(8,128)(2,1)S(1)} collective-permute-done((bf16[16,2,3,8,512]{4,3,0,1,2:T(8,128)(2,1)S(1)}, bf16[16,2,3,8,512]{4,3,0,1,2:T(8,128)(2,1)S(1)}, u32[]{:S(2)}, u32[]{:S(2)}) %collective-permute-start) | collective-permute-done | bytes 786464 | tf_op jit(solution)/shard_map/ppermute | solution.py:16
  96.3 0.9 fusion
  97.2 3.8 %fusion.25 = bf16[2,384,3,8,128]{1,4,2,0,3:T(8,128)(2,1)} fusion(bf16[2,384,3,512]{3,1,2,0:T(8,128)(2,1)S(1)} %fusion, s32[8,128]{1,0:T(8,128)S(1)} %get-tuple-element.49), kind=kOutput, calls=%fused_computation.52 | convolution fusion | flops 906166272 | bytes 5902336 | tf_op jit(solution)/shard_map/dot_general | solution.py:56
  101.0 3.8 %fusion.26 = bf16[2,384,3,8,128]{1,4,2,0,3:T(8,128)(2,1)} fusion(bf16[2,384,3,512]{3,1,2,0:T(8,128)(2,1)S(1)} %fusion, s32[8,128]{1,0:T(8,128)S(1)} %get-tuple-element.50), kind=kOutput, calls=%fused_computation.54 | convolution fusion | flops 906166272 | bytes 5902336 | tf_op jit(solution)/shard_map/dot_general | solution.py:56
  104.8 3.9 %fusion.27 = bf16[2,384,3,8,128]{1,4,3,2,0:T(8,128)(2,1)} fusion(bf16[2,384,3,512]{3,1,2,0:T(8,128)(2,1)S(1)} %fusion, s32[8,128]{1,0:T(8,128)S(1)} %iota_add_fusion.3), kind=kOutput, calls=%fused_computation.56 | convolution fusion | flops 906166272 | bytes 5902336 | tf_op jit(solution)/shard_map/dot_general | solution.py:56
  108.7 0.9 copy.332
  109.6 2.4 %collective-permute-start.1 = (bf16[2,384,3,64]{1,3,2,0:T(8,128)(2,1)}, bf16[2,384,3,64]{1,3,2,0:T(8,128)(2,1)}, u32[]{:S(2)}, u32[]{:S(2)}) collective-permute-start(bf16[2,384,3,64]{1,3,2,0:T(8,128)(2,1)} %copy.332), channel_id=1, source_target_pairs={{1,0},{2,1},{3,2},{4,3},{5,4},{6,5},{7,6},{8,7},{9,8},{10,9},{11,1... | collective-permute-start | bytes 884744 | tf_op jit(solution)/shard_map/ppermute | solution.py:16
  112.1 3.2 %fusion.35 = f32[2,384,3,128]{1,3,2,0:T(8,128)S(1)} fusion(bf16[2,384,3,8,128]{1,4,2,0,3:T(8,128)(2,1)} %fusion.25, f32[384]{0:T(512)} %copy-done.20, f32[384]{0:T(512)} %copy-done.23, f32[384]{0:T(512)S(1)} %get-tuple-element.8, f32[384]{0:T(512)S(1)} %get-tuple-element.9, f32[384]{0:T(512)S(1)} %get-tuple-element.10, f32[384]{0:T(512)} %copy-done.14, ...), kind=kLoop, calls=%fused_computation.75 | loop fusion | flops 6782976 | bytes 5910528 | tf_op jit(solution)/shard_map/add | solution.py:61
  115.3 1.9 %fusion.42 = f32[2,384,3,128]{1,3,2,0:T(8,128)} fusion(bf16[2,384,3,8,128]{1,4,2,0,3:T(8,128)(2,1)S(1)} %copy-done, f32[384]{0:T(512)S(1)} %copy-done.21, f32[384]{0:T(512)S(1)} %copy-done.24, f32[384]{0:T(512)S(1)} %get-tuple-element.8, f32[384]{0:T(512)S(1)} %get-tuple-element.9, f32[384]{0:T(512)S(1)} %get-tuple-element.10, f32[384]{0:T(512)S(1)} %copy-done.15, ...), kind=kLoop, calls=%fused_computation.90 | loop fusion | flops 6782976 | bytes 5910528 | tf_op jit(solution)/shard_map/add | solution.py:61
  117.3 0.8 copy-done.1
  118.1 1.9 %fusion.49 = f32[2,384,3,128]{1,3,2,0:T(8,128)} fusion(bf16[2,384,3,8,128]{1,4,3,2,0:T(8,128)(2,1)S(1)} %copy-done.1, f32[384]{0:T(512)S(1)} %copy-done.21, f32[384]{0:T(512)S(1)} %copy-done.24, f32[384]{0:T(512)S(1)} %get-tuple-element.8, f32[384]{0:T(512)S(1)} %get-tuple-element.9, f32[384]{0:T(512)S(1)} %get-tuple-element.10, f32[384]{0:T(512)S(1)} %copy-done.15, ...), kind=kLoop, calls=%fused_computation.105 | loop fusion | flops 6782976 | bytes 5910528 | tf_op jit(solution)/shard_map/add | solution.py:61
  120.0 3.7 %collective-permute-done.1 = bf16[2,384,3,64]{1,3,2,0:T(8,128)(2,1)} collective-permute-done((bf16[2,384,3,64]{1,3,2,0:T(8,128)(2,1)}, bf16[2,384,3,64]{1,3,2,0:T(8,128)(2,1)}, u32[]{:S(2)}, u32[]{:S(2)}) %collective-permute-start.1) | collective-permute-done | bytes 294944 | tf_op jit(solution)/shard_map/ppermute | solution.py:16
  123.7 2.0 %copy.333 = bf16[2,384,3,64]{3,1,2,0:T(8,128)(2,1)} copy(bf16[2,384,3,64]{1,3,2,0:T(8,128)(2,1)} %collective-permute-done.1) | data formatting | bytes 589824 | tf_op jit(solution)/shard_map/ppermute | solution.py:16
  125.7 2.7 %fusion.22 = bf16[2,384,3,8,128]{1,4,2,0,3:T(8,128)(2,1)S(1)} fusion(bf16[2,384,3,64]{3,1,2,0:T(8,128)(2,1)} %copy.333, bf16[2,384,3,512]{3,1,2,0:T(8,128)(2,1)S(1)} %fusion, s32[8,128]{1,0:T(8,128)} %copy-done.26), kind=kOutput, calls=%fused_computation.49 | convolution fusion | flops 907935744 | bytes 7376896 | tf_op jit(solution)/shard_map/dot_general | solution.py:56
  128.5 0.9 fusion.28
  131.0 3.1 %slice_bitcast_fusion.1 = (f32[384,4,512]{0,2,1:T(8,128)}, f32[384,4,512]{0,2,1:T(8,128)}) fusion(f32[2,384,4,512]{1,3,2,0:T(8,128)S(1)} %maximum_maximum_fusion), kind=kLoop, calls=%fused_computation.7 | loop fusion | bytes 12582912 | tf_op jit(solution)/shard_map/mul | solution.py:140
  134.1 2.4 %copy.399 = f32[384,4,512]{2,0,1:T(8,128)S(1)} copy(f32[384,4,512]{0,2,1:T(8,128)} %get-tuple-element.15) | data formatting | bytes 6291456 | tf_op jit(solution)/shard_map/mul | solution.py:140
  136.5 3.5 %copy.400 = f32[384,4,512]{2,0,1:T(8,128)} copy(f32[384,4,512]{0,2,1:T(8,128)} %get-tuple-element.16) | data formatting | bytes 6291456 | tf_op jit(solution)/shard_map/mul | solution.py:140
  140.0 6.6 %subtract_reduce_fusion = (bf16[384,4,512]{2,0,1:T(8,128)(2,1)S(1)}, bf16[384,4,512]{2,0,1:T(8,128)(2,1)S(1)}) fusion(f32[384,4,512]{2,0,1:T(8,128)} %copy.400, f32[384,4,4]{0,2,1:T(4,128)S(1)} %copy-done.28, f32[384,4,512]{2,0,1:T(8,128)S(1)} %copy.399, f32[384,4,4]{0,2,1:T(4,128)S(1)} %copy-done.27), kind=kLoop, calls=%fused_computation.1 | loop fusion | flops 23592960 | bytes 9486336 | tf_op jit(solution)/shard_map/reduce_sum | solution.py:140
  146.6 3.1 %fusion.4 = bf16[2,4,256,512]{3,2,1,0:T(8,128)(2,1)} fusion(bf16[1,384,4,512]{3,1,0,2:T(8,128)(2,1)S(1)} %bitcast.874, bf16[1,384,4,512]{3,1,0,2:T(8,128)(2,1)S(1)} %bitcast.873, bf16[1,256,2,384]{3,1,2,0:T(8,128)(2,1)S(1)} %copy-done.13, bf16[1,256,2,384]{3,1,2,0:T(8,128)(2,1)S(1)} %copy-done.12), kind=kOutput, calls=%fused_computation.13 | convolution fusion | flops 1619525632 | bytes 6029312 | tf_op jit(solution)/shard_map/dot_general | solution.py:37
  (96 shorter events, 7.6 us)
Async XLA Ops:
  3.7 10.9 %copy-start.4 = (bf16[2,4,8,16384]{3,2,1,0:T(8,128)(2,1)S(1)}, bf16[2,4,8,16384]{3,2,1,0:T(8,128)(2,1)}, u32[]{:S(2)}) copy-start(bf16[2,4,8,16384]{3,2,1,0:T(8,128)(2,1)} %param.6) | copy-start | bytes 6291460
  5.1 25.3 %all-to-all-start.1 = ((bf16[32,2,1,8,512]{4,3,1,2,0:T(8,128)(2,1)}), bf16[32,2,1,8,512]{4,3,1,2,0:T(8,128)(2,1)S(1)}, u32[]{:S(2)}, u32[]{:S(2)}) async-start(bf16[32,2,1,8,512]{4,3,1,2,0:T(8,128)(2,1)} %bitcast.871), calls=%async_computation.1 | async-start | bytes 1048576 | tf_op jit(solution)/shard_map/all_to_all | solution.py:116
  24.4 0.7 copy-start.32
  25.1 54.6 %copy-start.26 = (s32[8,128]{1,0:T(8,128)}, s32[8,128]{1,0:T(8,128)S(1)}, u32[]{:S(2)}) copy-start(s32[8,128]{1,0:T(8,128)S(1)} %iota_add_fusion) | copy-start | bytes 12292
  28.3 1.3 copy-start.30
  28.3 1.4 copy-start.31
  28.3 1.5 copy-start.29
  29.7 50.8 %copy-start.14 = (f32[384]{0:T(512)}, f32[384]{0:T(512)S(1)}, u32[]{:S(2)}) copy-start(f32[384]{0:T(512)S(1)} %get-tuple-element.11) | copy-start | bytes 4612
  29.7 50.8 %copy-start.17 = (f32[384]{0:T(512)}, f32[384]{0:T(512)S(1)}, u32[]{:S(2)}) copy-start(f32[384]{0:T(512)S(1)} %get-tuple-element.12) | copy-start | bytes 4612
  29.7 50.8 %copy-start.20 = (f32[384]{0:T(512)}, f32[384]{0:T(512)S(1)}, u32[]{:S(2)}) copy-start(f32[384]{0:T(512)S(1)} %get-tuple-element.13) | copy-start | bytes 4612
  29.7 50.8 %copy-start.23 = (f32[384]{0:T(512)}, f32[384]{0:T(512)S(1)}, u32[]{:S(2)}) copy-start(f32[384]{0:T(512)S(1)} %get-tuple-element.14) | copy-start | bytes 4612
  30.4 51.2 %all-to-all-start = ((bf16[32,2,3,8,512]{4,3,1,2,0:T(8,128)(2,1)}), bf16[32,2,3,8,512]{4,3,1,2,0:T(8,128)(2,1)S(1)}, u32[]{:S(2)}, u32[]{:S(2)}) async-start(bf16[32,2,3,8,512]{4,3,1,2,0:T(8,128)(2,1)} %copy.303), calls=%async_computation | async-start | bytes 3145728 | tf_op jit(solution)/shard_map/all_to_all | solution.py:116
  39.7 8.8 %collective-permute-start.2 = (bf16[16,2,1,8,512]{4,3,0,1,2:T(8,128)(2,1)S(1)}, bf16[16,2,1,8,512]{4,3,0,1,2:T(8,128)(2,1)S(1)}, u32[]{:S(2)}, u32[]{:S(2)}) collective-permute-start(bf16[16,2,1,8,512]{4,3,0,1,2:T(8,128)(2,1)S(1)} %copy.496), channel_id=1, source_target_pairs={{32,0},{64,32},{96,64},{128,96},{160,128},{192,160},{224,192},{33,... | collective-permute-start | bytes 786440 | tf_op jit(solution)/shard_map/ppermute | solution.py:16
  43.6 5.0 %copy-start.9 = (bf16[1,384,2,384]{1,3,2,0:T(8,128)(2,1)S(1)}, bf16[1,384,2,384]{1,3,2,0:T(8,128)(2,1)}, u32[]{:S(2)}) copy-start(bf16[1,384,2,384]{1,3,2,0:T(8,128)(2,1)} %get-tuple-element.26) | copy-start | bytes 1769476
  49.0 30.7 %collective-permute-start.3 = (bf16[2,384,1,64]{3,1,0,2:T(8,128)(2,1)S(1)}, bf16[2,384,1,64]{3,1,0,2:T(8,128)(2,1)S(1)}, u32[]{:S(2)}, u32[]{:S(2)}) collective-permute-start(bf16[2,384,1,64]{3,1,0,2:T(8,128)(2,1)S(1)} %slice.563), channel_id=1, source_target_pairs={{1,0},{2,1},{3,2},{4,3},{5,4},{6,5},{7,6},{8,7},{9,8},{10,9},{11,1... | collective-permute-start | bytes 294920 | tf_op jit(solution)/shard_map/ppermute | solution.py:16
  81.6 4.2 %copy-start.10 = (bf16[1,384,2,384]{1,3,2,0:T(8,128)(2,1)S(1)}, bf16[1,384,2,384]{1,3,2,0:T(8,128)(2,1)}, u32[]{:S(2)}) copy-start(bf16[1,384,2,384]{1,3,2,0:T(8,128)(2,1)} %get-tuple-element.26) | copy-start | bytes 1769476
  81.8 14.5 %copy-start.11 = (bf16[1,384,2,384]{1,3,2,0:T(8,128)(2,1)S(1)}, bf16[1,384,2,384]{1,3,2,0:T(8,128)(2,1)}, u32[]{:S(2)}) copy-start(bf16[1,384,2,384]{1,3,2,0:T(8,128)(2,1)} %get-tuple-element.26) | copy-start | bytes 1769476
  81.8 14.5 %collective-permute-start = (bf16[16,2,3,8,512]{4,3,0,1,2:T(8,128)(2,1)S(1)}, bf16[16,2,3,8,512]{4,3,0,1,2:T(8,128)(2,1)S(1)}, u32[]{:S(2)}, u32[]{:S(2)}) collective-permute-start(bf16[16,2,3,8,512]{4,3,0,1,2:T(8,128)(2,1)S(1)} %copy.497), channel_id=1, source_target_pairs={{32,0},{64,32},{96,64},{128,96},{160,128},{192,160},{224,192},{33,... | collective-permute-start | bytes 2359304 | tf_op jit(solution)/shard_map/ppermute | solution.py:16
  109.6 5.7 %copy-start = (bf16[2,384,3,8,128]{1,4,2,0,3:T(8,128)(2,1)S(1)}, bf16[2,384,3,8,128]{1,4,2,0,3:T(8,128)(2,1)}, u32[]{:S(2)}) copy-start(bf16[2,384,3,8,128]{1,4,2,0,3:T(8,128)(2,1)} %fusion.26) | copy-start | bytes 14155780
  109.6 5.7 %copy-start.15 = (f32[384]{0:T(512)S(1)}, f32[384]{0:T(512)}, u32[]{:S(2)}) copy-start(f32[384]{0:T(512)} %copy-done.14) | copy-start | bytes 4612
  109.6 5.7 %copy-start.18 = (f32[384]{0:T(512)S(1)}, f32[384]{0:T(512)}, u32[]{:S(2)}) copy-start(f32[384]{0:T(512)} %copy-done.17) | copy-start | bytes 4612
  109.6 5.7 %copy-start.21 = (f32[384]{0:T(512)S(1)}, f32[384]{0:T(512)}, u32[]{:S(2)}) copy-start(f32[384]{0:T(512)} %copy-done.20) | copy-start | bytes 4612
  109.6 5.7 %copy-start.24 = (f32[384]{0:T(512)S(1)}, f32[384]{0:T(512)}, u32[]{:S(2)}) copy-start(f32[384]{0:T(512)} %copy-done.23) | copy-start | bytes 4612
  109.6 14.0 %collective-permute-start.1 = (bf16[2,384,3,64]{1,3,2,0:T(8,128)(2,1)}, bf16[2,384,3,64]{1,3,2,0:T(8,128)(2,1)}, u32[]{:S(2)}, u32[]{:S(2)}) collective-permute-start(bf16[2,384,3,64]{1,3,2,0:T(8,128)(2,1)} %copy.332), channel_id=1, source_target_pairs={{1,0},{2,1},{3,2},{4,3},{5,4},{6,5},{7,6},{8,7},{9,8},{10,9},{11,1... | collective-permute-start | bytes 884744 | tf_op jit(solution)/shard_map/ppermute | solution.py:16
  115.3 2.8 %copy-start.1 = (bf16[2,384,3,8,128]{1,4,3,2,0:T(8,128)(2,1)S(1)}, bf16[2,384,3,8,128]{1,4,3,2,0:T(8,128)(2,1)}, u32[]{:S(2)}) copy-start(bf16[2,384,3,8,128]{1,4,3,2,0:T(8,128)(2,1)} %fusion.27) | copy-start | bytes 14155780
  125.7 2.7 %copy-start.16 = (f32[384]{0:T(512)S(1)}, f32[384]{0:T(512)}, u32[]{:S(2)}) copy-start(f32[384]{0:T(512)} %copy-done.14) | copy-start | bytes 4612
  125.7 2.7 %copy-start.19 = (f32[384]{0:T(512)S(1)}, f32[384]{0:T(512)}, u32[]{:S(2)}) copy-start(f32[384]{0:T(512)} %copy-done.17) | copy-start | bytes 4612
  125.7 2.7 %copy-start.22 = (f32[384]{0:T(512)S(1)}, f32[384]{0:T(512)}, u32[]{:S(2)}) copy-start(f32[384]{0:T(512)} %copy-done.20) | copy-start | bytes 4612
  125.7 2.7 %copy-start.25 = (f32[384]{0:T(512)S(1)}, f32[384]{0:T(512)}, u32[]{:S(2)}) copy-start(f32[384]{0:T(512)} %copy-done.23) | copy-start | bytes 4612
  128.5 1.3 copy-start.2
  128.5 1.6 %copy-start.3 = (f32[2,384,3,128]{1,3,2,0:T(8,128)S(1)}, f32[2,384,3,128]{1,3,2,0:T(8,128)}, u32[]{:S(2)}) copy-start(f32[2,384,3,128]{1,3,2,0:T(8,128)} %fusion.49) | copy-start | bytes 3538948
  128.5 1.7 %copy-start.5 = (f32[2,384,1,128]{1,3,2,0:T(8,128)S(1)}, f32[2,384,1,128]{1,3,2,0:T(8,128)}, u32[]{:S(2)}) copy-start(f32[2,384,1,128]{1,3,2,0:T(8,128)} %fusion.112) | copy-start | bytes 1179652
  128.5 1.8 %copy-start.6 = (f32[2,384,1,128]{1,3,2,0:T(8,128)S(1)}, f32[2,384,1,128]{1,3,2,0:T(8,128)}, u32[]{:S(2)}) copy-start(f32[2,384,1,128]{1,3,2,0:T(8,128)} %fusion.133) | copy-start | bytes 1179652
  128.5 1.9 %copy-start.7 = (f32[2,384,1,128]{1,3,2,0:T(8,128)S(1)}, f32[2,384,1,128]{1,3,2,0:T(8,128)}, u32[]{:S(2)}) copy-start(f32[2,384,1,128]{1,3,2,0:T(8,128)} %fusion.104) | copy-start | bytes 1179652
  128.5 2.0 %copy-start.8 = (f32[2,384,1,128]{1,3,2,0:T(8,128)S(1)}, f32[2,384,1,128]{1,3,2,0:T(8,128)}, u32[]{:S(2)}) copy-start(f32[2,384,1,128]{1,3,2,0:T(8,128)} %fusion.126) | copy-start | bytes 1179652
  136.4 3.5 %copy-start.27 = (f32[384,4,4]{0,2,1:T(4,128)S(1)}, f32[384,4,4]{0,2,1:T(4,128)}, u32[]{:S(2)}) copy-start(f32[384,4,4]{0,2,1:T(4,128)} %get-tuple-element.31) | copy-start | bytes 73732
  136.5 3.5 %copy-start.28 = (f32[384,4,4]{0,2,1:T(4,128)S(1)}, f32[384,4,4]{0,2,1:T(4,128)}, u32[]{:S(2)}) copy-start(f32[384,4,4]{0,2,1:T(4,128)} %get-tuple-element.32) | copy-start | bytes 73732
  140.0 6.6 %copy-start.12 = (bf16[1,256,2,384]{3,1,2,0:T(8,128)(2,1)S(1)}, bf16[1,256,2,384]{3,1,2,0:T(8,128)(2,1)}, u32[]{:S(2)}) copy-start(bf16[1,256,2,384]{3,1,2,0:T(8,128)(2,1)} %get-tuple-element.27) | copy-start | bytes 1179652
  140.0 6.6 %copy-start.13 = (bf16[1,256,2,384]{3,1,2,0:T(8,128)(2,1)S(1)}, bf16[1,256,2,384]{3,1,2,0:T(8,128)(2,1)}, u32[]{:S(2)}) copy-start(bf16[1,256,2,384]{3,1,2,0:T(8,128)(2,1)} %get-tuple-element.28) | copy-start | bytes 1179652

commit v4 on v2

--- a/solution.py
+++ b/solution.py
@@ -39,7 +39,7 @@
     )
 
 
-def migrate(extended, offsets, tap_weights, block):
+def migrate(spectra, border, offsets, tap_weights, block):
     tile = min(128, block)
     taps = tap_weights.shape[0]
     pieces = []
@@ -52,13 +52,18 @@
         onehot = (
             columns[None, None, :] == target[None, :, None] + tap_range[:, None, None]
         ).astype(jnp.bfloat16)
-        window_part = extended[:, :, :, first : first + tile + MARG]
+        if first + tile + MARG <= block:
+            window_part = spectra[:, :, :, first : first + tile + MARG]
+        else:
+            window_part = jnp.concatenate([spectra[:, :, :, first:], border], axis=3)
         picked = lax.dot_general(
             window_part, onehot, (((3,), (2,)), ((), ())), preferred_element_type=jnp.bfloat16
         )
         total = jnp.zeros(picked.shape[:3] + (tile,), jnp.float32)
         for tap_index in range(taps):
-            total = total + picked[:, :, :, tap_index].astype(jnp.float32) * tap_weights[tap_index][None, :, None, None]
+            total = total + picked[:, :, :, tap_index].astype(jnp.float32) * tap_weights[
+                tap_index
+            ][None, :, None, None]
         pieces.append(total)
     return jnp.concatenate(pieces, axis=3)
 
@@ -121,8 +126,7 @@
             + lax.dot_general(next_table, following, dims, preferred_element_type=jnp.float32)
         ).astype(jnp.bfloat16)
         border = shifted(spectra[:, :, :, :MARG], "dev", -1)
-        extended = jnp.concatenate([spectra, border], axis=3)
-        pieces.append(migrate(extended, offsets, tap_weights, block))
+        pieces.append(migrate(spectra, border, offsets, tap_weights, block))
     moved = jnp.concatenate(pieces, axis=2)
     mix_real = (
         azimuth_filter[0][:, None, :] * channel_mix[0]

time: 130 us -> 131 us (level)
  no operation moved by 1% of the time
where the time goes in v4:
time: 131 us; the launch traced here: 130 us
  waiting for transfers between devices  52.3 us (40%)
  starting transfers between devices  31.1 us (24%)
  other arithmetic  22.2 us (17%)
  matrix products  17.7 us (14%)
  local copies, waits for them, and re-layouts  6.52 us (5%)
    all_to_all x2, waiting for transfers between devices, body(): turned = lax.all_to_all(result, 'dev', 0, 0, tiled=True)  36.1 us
    all_to_all x2, starting transfers between devices, body(): turned = lax.all_to_all(result, 'dev', 0, 0, tiled=True)  16.4 us
    ppermute x4, waiting for transfers between devices, shifted(): return lax.ppermute(block, axis, route)  16.1 us
    ppermute x4, starting transfers between devices, shifted(): return lax.ppermute(block, axis, route)  14.7 us
    another operation x15, other arithmetic  12.8 us
    dot_general x8, matrix products, migrate(): lax.dot_general(window_part, onehot, (((3,), (2,)), ((), ())), preferred_...  8.27 us
    add x8, other arithmetic, migrate(): total + picked[:, :, :, tap_index].astype(jnp.float32) * tap_weights[tap_...  4.83 us
    dot_general x3, matrix products, apply_table(): lax.dot_general(table, data, (((2, 3), (part_dim, index_dim)), ((), ())),...  4.02 us
  transfers between devices with their start and end apart: 6, of which 5 were waited for; matrix products, arithmetic and copies ran while one was open for 17% of the time, Pallas kernels for 0%

profile of v4, /device:TPU:27, one launch (start us, length us, event | category | flops | bytes accessed | tf_op | source)
XLA Modules:
  0.0 130.3 jit_solution(15665144014735094867)
XLA Ops:
  0.8 1.1 fusion.173
  1.9 2.2 %fusion.120 = (bf16[2,8,128,128]{3,1,2,0:T(8,128)(2,1)S(1)}, bf16[2,8,128,128]{3,1,2,0:T(8,128)(2,1)S(1)}, bf16[2,8,128,128]{3,1,2,0:T(8,128)(2,1)S(1)}, bf16[2,8,128,128]{3,1,2,0:T(8,128)(2,1)S(1)}) fusion(f32[16384]{0:T(1024)S(1)} %get-tuple-element.60, f32[16384]{0:T(1024)S(1)} %get-tuple-element.59, bf16[2,4,8,16384]{3,2,1,0:T(8,128)(2,1)} %param.6), kind=kLoop, calls=%fused_computation.244 | loop fusion | flops 5242880 | bytes 4325376
  5.5 0.6 subtract_convert_fusion
  6.1 0.5 fusion.7
  7.0 1.1 copy.211
  8.2 10.9 %all-to-all-start.1 = ((bf16[32,2,2,8,512]{4,3,1,2,0:T(8,128)(2,1)}), bf16[32,2,2,8,512]{4,3,1,2,0:T(8,128)(2,1)S(1)}, u32[]{:S(2)}, u32[]{:S(2)}) async-start(bf16[32,2,2,8,512]{4,3,1,2,0:T(8,128)(2,1)} %copy.211), calls=%async_computation.1 | async-start | bytes 2097152 | tf_op jit(solution)/shard_map/all_to_all | solution.py:122
  19.1 0.5 fusion.6
  20.0 1.1 copy.170
  21.1 25.1 %all-to-all-done.1 = bf16[32,2,2,8,512]{4,3,1,2,0:T(8,128)(2,1)S(1)} async-done(((bf16[32,2,2,8,512]{4,3,1,2,0:T(8,128)(2,1)}), bf16[32,2,2,8,512]{4,3,1,2,0:T(8,128)(2,1)S(1)}, u32[]{:S(2)}, u32[]{:S(2)}) %all-to-all-start.1) | async-done | bytes 1048608 | tf_op jit(solution)/shard_map/all_to_all | solution.py:122
  46.2 5.5 %all-to-all-start = ((bf16[32,2,2,8,512]{4,3,1,2,0:T(8,128)(2,1)}), bf16[32,2,2,8,512]{4,3,1,2,0:T(8,128)(2,1)S(1)}, u32[]{:S(2)}, u32[]{:S(2)}) async-start(bf16[32,2,2,8,512]{4,3,1,2,0:T(8,128)(2,1)} %copy.170), calls=%async_computation | async-start | bytes 2097152 | tf_op jit(solution)/shard_map/all_to_all | solution.py:122
  51.9 1.5 %fusion.139 = bf16[256,1,384]{2,0,1:T(8,128)(2,1)S(1)} fusion(), kind=kLoop, calls=%fused_computation.338 | loop fusion | flops 1081344 | bytes 196608 | tf_op jit(solution)/shard_map/convert.107
  53.5 2.3 %fusion.118 = bf16[384,1,384]{0,2,1:T(8,128)(2,1)S(1)} fusion(), kind=kLoop, calls=%fused_computation.242 | loop fusion | flops 1622016 | bytes 294912 | tf_op jit(solution)/shard_map/convert.99
  55.8 1.7 %negate_convert_fusion.1 = (bf16[256,1,384]{2,0,1:T(8,128)(2,1)S(1)}, bf16[256,1,384]{2,0,1:T(8,128)(2,1)S(1)}) fusion(), kind=kLoop, calls=%fused_computation.331 | loop fusion | flops 1376256 | bytes 393216 | tf_op jit(solution)/shard_map/convert.111
  57.5 2.6 %negate_convert_fusion = (bf16[384,1,384]{0,2,1:T(8,128)(2,1)S(1)}, bf16[384,1,384]{0,2,1:T(8,128)(2,1)S(1)}) fusion(), kind=kLoop, calls=%fused_computation.235 | loop fusion | flops 2064384 | bytes 589824 | tf_op jit(solution)/shard_map/convert.103
  60.1 1.0 maximum_bitcast_fusion.18
  61.3 0.8 copy.342
  62.2 4.2 %collective-permute-start.2 = (bf16[16,2,2,8,512]{4,3,0,1,2:T(8,128)(2,1)}, bf16[16,2,2,8,512]{4,3,0,1,2:T(8,128)(2,1)}, u32[]{:S(2)}, u32[]{:S(2)}) collective-permute-start(bf16[16,2,2,8,512]{4,3,0,1,2:T(8,128)(2,1)} %copy.342), channel_id=1, source_target_pairs={{32,0},{64,32},{96,64},{128,96},{160,128},{192,160},{224,192},{33,... | collective-permute-start | bytes 1572872 | tf_op jit(solution)/shard_map/ppermute | solution.py:16
  66.3 11.1 %all-to-all-done = bf16[32,2,2,8,512]{4,3,1,2,0:T(8,128)(2,1)S(1)} async-done(((bf16[32,2,2,8,512]{4,3,1,2,0:T(8,128)(2,1)}), bf16[32,2,2,8,512]{4,3,1,2,0:T(8,128)(2,1)S(1)}, u32[]{:S(2)}, u32[]{:S(2)}) %all-to-all-start) | async-done | bytes 1048608 | tf_op jit(solution)/shard_map/all_to_all | solution.py:122
  77.5 5.6 %collective-permute-start = (bf16[16,2,2,8,512]{4,3,0,1,2:T(8,128)(2,1)S(1)}, bf16[16,2,2,8,512]{4,3,0,1,2:T(8,128)(2,1)S(1)}, u32[]{:S(2)}, u32[]{:S(2)}) collective-permute-start(bf16[16,2,2,8,512]{4,3,0,1,2:T(8,128)(2,1)S(1)} %copy.341), channel_id=1, source_target_pairs={{32,0},{64,32},{96,64},{128,96},{160,128},{192,160},{224,192},{33,... | collective-permute-start | bytes 1572872 | tf_op jit(solution)/shard_map/ppermute | solution.py:16
  83.1 1.0 fusion.20
  84.2 1.1 fusion.23
  85.3 1.7 %fusion.3 = bf16[2,384,2,512]{3,1,2,0:T(8,128)(2,1)S(1)} fusion(f32[2,384,2,512,1,1]{3,1,5,4,2,0:T(8,128)S(1)} %fusion.20, bf16[16,2,2,8,512]{4,3,0,1,2:T(8,128)(2,1)} %collective-permute-done.2, bf16[1,384,2,384]{1,3,2,0:T(8,128)(2,1)S(1)} %get-tuple-element.53, bf16[1,384,2,384]{1,3,2,0:T(8,128)(2,1)S(1)} %get-tuple-element.54), kind=kOutput, calls=%fused_computation.8 | convolution fusion | flops 405012480 | bytes 6422528 | tf_op jit(solution)/shard_map/dot_general | solution.py:126
  87.1 3.8 %collective-permute-done = bf16[16,2,2,8,512]{4,3,0,1,2:T(8,128)(2,1)S(1)} collective-permute-done((bf16[16,2,2,8,512]{4,3,0,1,2:T(8,128)(2,1)S(1)}, bf16[16,2,2,8,512]{4,3,0,1,2:T(8,128)(2,1)S(1)}, u32[]{:S(2)}, u32[]{:S(2)}) %collective-permute-start) | collective-permute-done | bytes 524320 | tf_op jit(solution)/shard_map/ppermute | solution.py:16
  90.9 0.7 fusion.4
  91.6 1.0 fusion.28
  92.7 1.0 fusion.31
  93.7 1.0 fusion.29
  94.8 1.0 fusion.32
  95.8 1.0 fusion.30
  96.9 1.0 fusion.33
  97.9 2.5 %collective-permute-start.3 = (bf16[2,384,2,64]{3,1,2,0:T(8,128)(2,1)S(1)}, bf16[2,384,2,64]{3,1,2,0:T(8,128)(2,1)S(1)}, u32[]{:S(2)}, u32[]{:S(2)}) collective-permute-start(bf16[2,384,2,64]{3,1,2,0:T(8,128)(2,1)S(1)} %slice.780), channel_id=1, source_target_pairs={{1,0},{2,1},{3,2},{4,3},{5,4},{6,5},{7,6},{8,7},{9,8},{10,9},{11,1... | collective-permute-start | bytes 589832 | tf_op jit(solution)/shard_map/ppermute | solution.py:16
  100.4 0.6 fusion.51
  101.0 0.6 fusion.58
  101.6 0.6 fusion.65
  102.2 2.4 %collective-permute-start.1 = (bf16[2,384,2,64]{3,1,2,0:T(8,128)(2,1)S(1)}, bf16[2,384,2,64]{3,1,2,0:T(8,128)(2,1)S(1)}, u32[]{:S(2)}, u32[]{:S(2)}) collective-permute-start(bf16[2,384,2,64]{3,1,2,0:T(8,128)(2,1)S(1)} %slice.732), channel_id=1, source_target_pairs={{1,0},{2,1},{3,2},{4,3},{5,4},{6,5},{7,6},{8,7},{9,8},{10,9},{11,1... | collective-permute-start | bytes 589832 | tf_op jit(solution)/shard_map/ppermute | solution.py:16
  104.6 0.6 fusion.79
  105.2 0.6 fusion.86
  105.8 0.6 fusion.93
  106.5 6.6 %collective-permute-done.3 = bf16[2,384,2,64]{3,1,2,0:T(8,128)(2,1)S(1)} collective-permute-done((bf16[2,384,2,64]{3,1,2,0:T(8,128)(2,1)S(1)}, bf16[2,384,2,64]{3,1,2,0:T(8,128)(2,1)S(1)}, u32[]{:S(2)}, u32[]{:S(2)}) %collective-permute-start.3) | collective-permute-done | bytes 196640 | tf_op jit(solution)/shard_map/ppermute | solution.py:16
  113.0 1.0 fusion.41
  114.1 0.6 fusion.44
  114.7 5.7 %collective-permute-done.1 = bf16[2,384,2,64]{3,1,2,0:T(8,128)(2,1)S(1)} collective-permute-done((bf16[2,384,2,64]{3,1,2,0:T(8,128)(2,1)S(1)}, bf16[2,384,2,64]{3,1,2,0:T(8,128)(2,1)S(1)}, u32[]{:S(2)}, u32[]{:S(2)}) %collective-permute-start.1) | collective-permute-done | bytes 196640 | tf_op jit(solution)/shard_map/ppermute | solution.py:16
  120.4 1.0 fusion.38
  121.5 0.6 fusion.72
  123.4 0.4 subtract_convert_fusion.4
  124.2 0.4 subtract_convert_fusion.3
  126.5 0.5 copy-done.2
  127.1 3.1 %fusion.5 = bf16[2,4,256,512]{3,2,1,0:T(8,128)(2,1)} fusion(bf16[1,384,4,512]{1,3,2,0:T(8,128)(2,1)S(1)} %maximum_bitcast_fusion.5, bf16[1,384,4,512]{1,3,2,0:T(8,128)(2,1)S(1)} %maximum_bitcast_fusion.4, bf16[1,256,2,384]{3,1,2,0:T(8,128)(2,1)S(1)} %copy-done.3, bf16[1,256,2,384]{3,1,2,0:T(8,128)(2,1)S(1)} %copy-done.2), kind=kOutput, calls=%fused_computation.11 | convolution fusion | flops 1619525632 | bytes 6029312 | tf_op jit(solution)/shard_map/dot_general | solution.py:37
  (56 shorter events, 7.3 us)
Async XLA Ops:
  8.2 38.0 %all-to-all-start.1 = ((bf16[32,2,2,8,512]{4,3,1,2,0:T(8,128)(2,1)}), bf16[32,2,2,8,512]{4,3,1,2,0:T(8,128)(2,1)S(1)}, u32[]{:S(2)}, u32[]{:S(2)}) async-start(bf16[32,2,2,8,512]{4,3,1,2,0:T(8,128)(2,1)} %copy.211), calls=%async_computation.1 | async-start | bytes 2097152 | tf_op jit(solution)/shard_map/all_to_all | solution.py:122
  19.1 2.0 %copy-start.6 = (f32[2,4,384]{2,1,0:T(4,128)S(1)}, f32[2,4,384]{2,1,0:T(4,128)}, u32[]{:S(2)}) copy-start(f32[2,4,384]{2,1,0:T(4,128)} %param.11) | copy-start | bytes 36868
  19.6 32.1 %copy-start.4 = (f32[2,4,4,384]{3,2,1,0:T(4,128)S(1)}, f32[2,4,4,384]{3,2,1,0:T(4,128)}, u32[]{:S(2)}) copy-start(f32[2,4,4,384]{3,2,1,0:T(4,128)} %param.10) | copy-start | bytes 147460
  19.6 32.1 %copy-start.5 = (f32[8,384]{1,0:T(8,128)S(1)}, f32[8,384]{1,0:T(8,128)}, u32[]{:S(2)}) copy-start(f32[8,384]{1,0:T(8,128)} %param.9) | copy-start | bytes 36868
  21.1 40.1 %copy-start.7 = (s32[512]{0:T(512)S(1)}, s32[512]{0:T(512)}, u32[]{:S(2)}) copy-start(s32[512]{0:T(512)} %param.8) | copy-start | bytes 6148
  46.2 31.2 %all-to-all-start = ((bf16[32,2,2,8,512]{4,3,1,2,0:T(8,128)(2,1)}), bf16[32,2,2,8,512]{4,3,1,2,0:T(8,128)(2,1)S(1)}, u32[]{:S(2)}, u32[]{:S(2)}) async-start(bf16[32,2,2,8,512]{4,3,1,2,0:T(8,128)(2,1)} %copy.170), calls=%async_computation | async-start | bytes 2097152 | tf_op jit(solution)/shard_map/all_to_all | solution.py:122
  62.2 23.1 %collective-permute-start.2 = (bf16[16,2,2,8,512]{4,3,0,1,2:T(8,128)(2,1)}, bf16[16,2,2,8,512]{4,3,0,1,2:T(8,128)(2,1)}, u32[]{:S(2)}, u32[]{:S(2)}) collective-permute-start(bf16[16,2,2,8,512]{4,3,0,1,2:T(8,128)(2,1)} %copy.342), channel_id=1, source_target_pairs={{32,0},{64,32},{96,64},{128,96},{160,128},{192,160},{224,192},{33,... | collective-permute-start | bytes 1572872 | tf_op jit(solution)/shard_map/ppermute | solution.py:16
  77.5 13.4 %collective-permute-start = (bf16[16,2,2,8,512]{4,3,0,1,2:T(8,128)(2,1)S(1)}, bf16[16,2,2,8,512]{4,3,0,1,2:T(8,128)(2,1)S(1)}, u32[]{:S(2)}, u32[]{:S(2)}) collective-permute-start(bf16[16,2,2,8,512]{4,3,0,1,2:T(8,128)(2,1)S(1)} %copy.341), channel_id=1, source_target_pairs={{32,0},{64,32},{96,64},{128,96},{160,128},{192,160},{224,192},{33,... | collective-permute-start | bytes 1572872 | tf_op jit(solution)/shard_map/ppermute | solution.py:16
  87.0 8.8 %copy-start.1 = (bf16[2,384,2,512]{3,1,2,0:T(8,128)(2,1)}, bf16[2,384,2,512]{3,1,2,0:T(8,128)(2,1)S(1)}, u32[]{:S(2)}) copy-start(bf16[2,384,2,512]{3,1,2,0:T(8,128)(2,1)S(1)} %fusion.3) | copy-start | bytes 4718596
  91.5 5.3 %copy-start = (bf16[2,384,2,512]{3,1,2,0:T(8,128)(2,1)}, bf16[2,384,2,512]{3,1,2,0:T(8,128)(2,1)S(1)}, u32[]{:S(2)}) copy-start(bf16[2,384,2,512]{3,1,2,0:T(8,128)(2,1)S(1)} %fusion.4) | copy-start | bytes 4718596
  97.9 15.1 %collective-permute-start.3 = (bf16[2,384,2,64]{3,1,2,0:T(8,128)(2,1)S(1)}, bf16[2,384,2,64]{3,1,2,0:T(8,128)(2,1)S(1)}, u32[]{:S(2)}, u32[]{:S(2)}) collective-permute-start(bf16[2,384,2,64]{3,1,2,0:T(8,128)(2,1)S(1)} %slice.780), channel_id=1, source_target_pairs={{1,0},{2,1},{3,2},{4,3},{5,4},{6,5},{7,6},{8,7},{9,8},{10,9},{11,1... | collective-permute-start | bytes 589832 | tf_op jit(solution)/shard_map/ppermute | solution.py:16
  102.2 18.2 %collective-permute-start.1 = (bf16[2,384,2,64]{3,1,2,0:T(8,128)(2,1)S(1)}, bf16[2,384,2,64]{3,1,2,0:T(8,128)(2,1)S(1)}, u32[]{:S(2)}, u32[]{:S(2)}) collective-permute-start(bf16[2,384,2,64]{3,1,2,0:T(8,128)(2,1)S(1)} %slice.732), channel_id=1, source_target_pairs={{1,0},{2,1},{3,2},{4,3},{5,4},{6,5},{7,6},{8,7},{9,8},{10,9},{11,1... | collective-permute-start | bytes 589832 | tf_op jit(solution)/shard_map/ppermute | solution.py:16
  105.2 7.8 %slice-start.1 = ((bf16[2,384,2,512]{3,1,2,0:T(8,128)(2,1)}), bf16[2,384,2,128]{3,1,2,0:T(8,128)(2,1)S(1)}, s32[]{:S(2)}) async-start(bf16[2,384,2,512]{3,1,2,0:T(8,128)(2,1)} %copy-done.1), calls=%async_computation.3 | async-start | bytes 786432 | tf_op jit(solution)/shard_map/slice | solution.py:58
  106.4 14.0 %slice-start = ((bf16[2,384,2,512]{3,1,2,0:T(8,128)(2,1)}), bf16[2,384,2,128]{3,1,2,0:T(8,128)(2,1)S(1)}, s32[]{:S(2)}) async-start(bf16[2,384,2,512]{3,1,2,0:T(8,128)(2,1)} %copy-done), calls=%async_computation.2 | async-start | bytes 786432 | tf_op jit(solution)/shard_map/slice | solution.py:58
  126.0 1.0 copy-start.2
  126.0 1.1 copy-start.3

commit v5 on v4

--- a/solution.py
+++ b/solution.py
@@ -55,7 +55,9 @@
         if first + tile + MARG <= block:
             window_part = spectra[:, :, :, first : first + tile + MARG]
         else:
-            window_part = jnp.concatenate([spectra[:, :, :, first:], border], axis=3)
+            window_part = jnp.concatenate(
+                [spectra[:, :, :, first:], border[:, :, :, :MARG]], axis=3
+            )
         picked = lax.dot_general(
             window_part, onehot, (((3,), (2,)), ((), ())), preferred_element_type=jnp.bfloat16
         )
@@ -68,7 +70,7 @@
     return jnp.concatenate(pieces, axis=3)
 
 
-CHUNKS = 2
+CHUNKS = 1
 
 
 def compress_block(echoes, range_phase, dev_count):
@@ -125,7 +127,7 @@
             lax.dot_general(own_table, turned, dims, preferred_element_type=jnp.float32)
             + lax.dot_general(next_table, following, dims, preferred_element_type=jnp.float32)
         ).astype(jnp.bfloat16)
-        border = shifted(spectra[:, :, :, :MARG], "dev", -1)
+        border = shifted(spectra[:, :, :, : 2 * MARG], "dev", -1)
         pieces.append(migrate(spectra, border, offsets, tap_weights, block))
     moved = jnp.concatenate(pieces, axis=2)
     mix_real = (

time: 131 us -> 123 us (0.939)
  starting transfers between devices: 31.1 us -> 16.2 us
  waiting for transfers between devices: 52.3 us -> 63 us
  matrix products: 17.7 us -> 14.9 us
    ppermute x4 -> x2, starting transfers between devices: 14.7 us -> 5.17 us  [shifted(): return lax.ppermute(block, axis, route)]
    ppermute x4 -> x2, waiting for transfers between devices: 16.1 us -> 22.3 us  [shifted(): return lax.ppermute(block, axis, route)]
    all_to_all x2 -> x1, starting transfers between devices: 16.4 us -> 11 us  [body(): turned = lax.all_to_all(result, 'dev', 0, 0, tiled=True)]
    all_to_all x2 -> x1, waiting for transfers between devices: 36.1 us -> 40.8 us  [body(): turned = lax.all_to_all(result, 'dev', 0, 0, tiled=True)]
    dot_general x8 -> x4, matrix products: 8.27 us -> 7.38 us  [migrate(): lax.dot_general(window_part, onehot, (((3,), (2,)), ((), ())), preferred_...]
    add x8 -> x4, other arithmetic: 4.83 us -> 5.07 us  [migrate(): total + picked[:, :, :, tap_index].astype(jnp.float32) * tap_weights[tap_...]
    dot_general x3 -> x2, matrix products: 4.02 us -> 3.87 us  [apply_table(): lax.dot_general(table, data, (((2, 3), (part_dim, index_dim)), ((), ())),...]
  transfers between devices with their start and end apart: 6 -> 3, of which waited for: 5 -> 3; matrix products, arithmetic and copies ran while one was open for 17% -> 17% of each run, Pallas kernels for 0% -> 0%
where the time goes in v5:
time: 123 us
  waiting for transfers between devices  63 us (51%)
  other arithmetic  22.5 us (18%)
  starting transfers between devices  16.2 us (13%)
  matrix products  14.9 us (12%)
  local copies, waits for them, and re-layouts  5.7 us (5%)
    all_to_all x1, waiting for transfers between devices, body(): turned = lax.all_to_all(result, 'dev', 0, 0, tiled=True)  40.8 us
    ppermute x2, waiting for transfers between devices, shifted(): return lax.ppermute(block, axis, route)  22.3 us
    another operation x15, other arithmetic  12.8 us
    all_to_all x1, starting transfers between devices, body(): turned = lax.all_to_all(result, 'dev', 0, 0, tiled=True)  11 us
    dot_general x4, matrix products, migrate(): lax.dot_general(window_part, onehot, (((3,), (2,)), ((), ())), preferred_...  7.38 us
    ppermute x2, starting transfers between devices, shifted(): return lax.ppermute(block, axis, route)  5.17 us
    add x4, other arithmetic, migrate(): total + picked[:, :, :, tap_index].astype(jnp.float32) * tap_weights[tap_...  5.07 us
    dot_general x2, matrix products, apply_table(): lax.dot_general(table, data, (((2, 3), (part_dim, index_dim)), ((), ())),...  3.87 us
  transfers between devices with their start and end apart: 3, of which 3 were waited for; matrix products, arithmetic and copies ran while one was open for 17% of the time, Pallas kernels for 0%

profile of v5, /device:TPU:27, one launch (start us, length us, event | category | flops | bytes accessed | tf_op | source)
XLA Modules:
  0.0 122.8 jit_solution(1930643512804198591)
XLA Ops:
  0.0 0.3 negate_convert_fusion.2
  0.3 0.3 fusion.103
  0.5 0.3 sine_multiply_fusion.2
  0.8 1.1 fusion.113
  1.9 2.2 %fusion.52 = (bf16[4,8,128,128]{3,1,2,0:T(8,128)(2,1)S(1)}, bf16[4,8,128,128]{3,1,2,0:T(8,128)(2,1)S(1)}) fusion(f32[16384]{0:T(1024)S(1)} %get-tuple-element.56, f32[16384]{0:T(1024)S(1)} %get-tuple-element.55, bf16[2,4,8,16384]{3,2,1,0:T(8,128)(2,1)} %param.6), kind=kLoop, calls=%fused_computation.105 | loop fusion | flops 5242880 | bytes 4325376
  4.1 0.6 copy_bitcast_fusion.1
  4.8 0.7 convolution_bitcast_fusion
  5.5 0.6 subtract_convert_fusion
  6.1 0.7 fusion.14
  6.9 0.8 copy.186
  7.7 1.6 %copy.90 = bf16[32,2,4,8,512]{4,3,1,2,0:T(8,128)(2,1)} copy(bf16[32,2,4,8,512]{4,3,2,1,0:T(8,128)(2,1)S(1)} %bitcast.486) | data formatting | bytes 4194304 | tf_op jit(solution)/shard_map/reshape | solution.py:105
  9.3 11.0 %all-to-all-start = ((bf16[32,2,4,8,512]{4,3,1,2,0:T(8,128)(2,1)}), bf16[32,2,4,8,512]{4,3,1,2,0:T(8,128)(2,1)S(1)}, u32[]{:S(2)}, u32[]{:S(2)}) async-start(bf16[32,2,4,8,512]{4,3,1,2,0:T(8,128)(2,1)} %copy.90), calls=%async_computation | async-start | bytes 4194304 | tf_op jit(solution)/shard_map/all_to_all | solution.py:124
  20.6 1.5 %fusion.87 = bf16[256,1,384]{2,0,1:T(8,128)(2,1)S(1)} fusion(), kind=kLoop, calls=%fused_computation.203 | loop fusion | flops 1081344 | bytes 196608 | tf_op jit(solution)/shard_map/convert.69
  22.1 2.3 %fusion.74 = bf16[384,1,384]{0,2,1:T(8,128)(2,1)S(1)} fusion(), kind=kLoop, calls=%fused_computation.184 | loop fusion | flops 1622016 | bytes 294912 | tf_op jit(solution)/shard_map/convert.61
  24.5 1.7 %negate_convert_fusion.1 = (bf16[256,1,384]{2,0,1:T(8,128)(2,1)S(1)}, bf16[256,1,384]{2,0,1:T(8,128)(2,1)S(1)}) fusion(), kind=kLoop, calls=%fused_computation.196 | loop fusion | flops 1376256 | bytes 393216 | tf_op jit(solution)/shard_map/convert.73
  26.2 2.6 %negate_convert_fusion = (bf16[384,1,384]{0,2,1:T(8,128)(2,1)S(1)}, bf16[384,1,384]{0,2,1:T(8,128)(2,1)S(1)}) fusion(), kind=kLoop, calls=%fused_computation.177 | loop fusion | flops 2064384 | bytes 589824 | tf_op jit(solution)/shard_map/convert.65
  28.8 1.0 maximum_bitcast_fusion.13
  29.8 0.1 maximum_bitcast_fusion.12
  30.0 40.8 %all-to-all-done = bf16[32,2,4,8,512]{4,3,1,2,0:T(8,128)(2,1)S(1)} async-done(((bf16[32,2,4,8,512]{4,3,1,2,0:T(8,128)(2,1)}), bf16[32,2,4,8,512]{4,3,1,2,0:T(8,128)(2,1)S(1)}, u32[]{:S(2)}, u32[]{:S(2)}) %all-to-all-start) | async-done | bytes 2097184 | tf_op jit(solution)/shard_map/all_to_all | solution.py:124
  70.9 2.7 %collective-permute-start = (bf16[16,2,4,8,512]{4,3,0,1,2:T(8,128)(2,1)S(1)}, bf16[16,2,4,8,512]{4,3,0,1,2:T(8,128)(2,1)S(1)}, u32[]{:S(2)}, u32[]{:S(2)}) collective-permute-start(bf16[16,2,4,8,512]{4,3,0,1,2:T(8,128)(2,1)S(1)} %copy.185), channel_id=1, source_target_pairs={{32,0},{64,32},{96,64},{128,96},{160,128},{192,160},{224,192},{33,... | collective-permute-start | bytes 3145736 | tf_op jit(solution)/shard_map/ppermute | solution.py:16
  73.6 1.9 %fusion.11 = f32[2,384,4,512,1,1]{3,1,5,4,2,0:T(8,128)S(1)} fusion(bf16[1,384,2,384]{1,3,2,0:T(8,128)(2,1)S(1)} %get-tuple-element.52, bf16[1,384,2,384]{1,3,2,0:T(8,128)(2,1)S(1)} %get-tuple-element.51, bf16[32,2,4,8,512]{4,3,1,2,0:T(8,128)(2,1)S(1)} %all-to-all-done), kind=kOutput, calls=%fused_computation.23 | convolution fusion | flops 1612185600 | bytes 9568256 | tf_op jit(solution)/shard_map/dot_general | solution.py:127
  75.5 11.5 %collective-permute-done = bf16[16,2,4,8,512]{4,3,0,1,2:T(8,128)(2,1)S(1)} collective-permute-done((bf16[16,2,4,8,512]{4,3,0,1,2:T(8,128)(2,1)S(1)}, bf16[16,2,4,8,512]{4,3,0,1,2:T(8,128)(2,1)S(1)}, u32[]{:S(2)}, u32[]{:S(2)}) %collective-permute-start) | collective-permute-done | bytes 1048608 | tf_op jit(solution)/shard_map/ppermute | solution.py:16
  87.0 1.1 fusion
  88.1 0.4 fusion.112
  88.5 2.5 %collective-permute-start.1 = (bf16[2,384,4,128]{3,1,2,0:T(8,128)(2,1)S(1)}, bf16[2,384,4,128]{3,1,2,0:T(8,128)(2,1)S(1)}, u32[]{:S(2)}, u32[]{:S(2)}) collective-permute-start(bf16[2,384,4,128]{3,1,2,0:T(8,128)(2,1)S(1)} %get-tuple-element.48), channel_id=1, source_target_pairs={{1,0},{2,1},{3,2},{4,3},{5,4},{6,5},{7,6},{8,7},{9,8},{10,9},{11,1... | collective-permute-start | bytes 2359304 | tf_op jit(solution)/shard_map/ppermute | solution.py:16
  91.0 1.8 %fusion.17 = bf16[2,384,4,8,128]{1,4,2,0,3:T(8,128)(2,1)S(1)} fusion(bf16[2,384,4,512]{3,1,2,0:T(8,128)(2,1)S(1)} %fusion, s32[8,128]{1,0:T(8,128)S(1)} %get-tuple-element.75), kind=kOutput, calls=%fused_computation.31 | convolution fusion | flops 1208156160 | bytes 7868416 | tf_op jit(solution)/shard_map/dot_general | solution.py:61
  92.8 1.8 %fusion.18 = bf16[2,384,4,8,128]{1,4,2,0,3:T(8,128)(2,1)S(1)} fusion(bf16[2,384,4,512]{3,1,2,0:T(8,128)(2,1)S(1)} %fusion, s32[8,128]{1,0:T(8,128)S(1)} %get-tuple-element.76), kind=kOutput, calls=%fused_computation.33 | convolution fusion | flops 1208156160 | bytes 7868416 | tf_op jit(solution)/shard_map/dot_general | solution.py:61
  94.7 1.2 fusion.30
  95.9 1.2 fusion.37
  97.1 1.8 %fusion.19 = bf16[2,384,4,8,128]{1,4,3,2,0:T(8,128)(2,1)S(1)} fusion(bf16[2,384,4,512]{3,1,2,0:T(8,128)(2,1)S(1)} %fusion, s32[8,128]{1,0:T(8,128)S(1)} %iota_add_fusion.3), kind=kOutput, calls=%fused_computation.35 | convolution fusion | flops 1208156160 | bytes 7868416 | tf_op jit(solution)/shard_map/dot_general | solution.py:61
  99.0 1.2 fusion.44
  100.2 10.8 %collective-permute-done.1 = bf16[2,384,4,128]{3,1,2,0:T(8,128)(2,1)S(1)} collective-permute-done((bf16[2,384,4,128]{3,1,2,0:T(8,128)(2,1)S(1)}, bf16[2,384,4,128]{3,1,2,0:T(8,128)(2,1)S(1)}, u32[]{:S(2)}, u32[]{:S(2)}) %collective-permute-start.1) | collective-permute-done | bytes 786464 | tf_op jit(solution)/shard_map/ppermute | solution.py:16
  111.0 1.8 %fusion.20 = bf16[2,384,4,8,128]{1,4,2,0,3:T(8,128)(2,1)S(1)} fusion(bf16[2,384,4,64]{3,1,2,0:T(8,128)(2,1)S(1)} %bitcast.487, bf16[2,384,4,128]{3,1,2,0:T(8,128)(2,1)S(1)} %get-tuple-element.47, s32[8,128]{1,0:T(8,128)S(1)} %iota_add_fusion), kind=kOutput, calls=%fused_computation.37 | convolution fusion | flops 1210515456 | bytes 7475200 | tf_op jit(solution)/shard_map/dot_general | solution.py:61
  112.8 1.4 %fusion.23 = f32[2,384,4,128]{1,3,2,0:T(8,128)S(1)} fusion(bf16[2,384,4,8,128]{1,4,2,0,3:T(8,128)(2,1)S(1)} %fusion.20, f32[384]{0:T(512)S(1)} %get-tuple-element.43, f32[384]{0:T(512)S(1)} %get-tuple-element.44, f32[384]{0:T(512)S(1)} %get-tuple-element.38, f32[384]{0:T(512)S(1)} %get-tuple-element.39, f32[384]{0:T(512)S(1)} %get-tuple-element.40, ...), kind=kLoop, calls=%fused_computation.43 | loop fusion | flops 9043968 | bytes 7876608 | tf_op jit(solution)/shard_map/add | solution.py:66
  114.3 0.5 pad_maximum_fusion
  114.7 0.4 subtract_convert_fusion.3
  115.2 0.4 add_convert_fusion.3
  115.6 0.4 subtract_convert_fusion.4
  116.1 0.4 add_convert_fusion.4
  116.5 0.4 subtract_convert_fusion.2
  116.9 0.4 add_convert_fusion.2
  117.4 0.4 subtract_convert_fusion.1
  117.8 0.4 add_convert_fusion.1
  118.2 0.2 maximum_bitcast_fusion.9
  118.5 0.2 maximum_bitcast_fusion.10
  118.8 0.7 copy-done
  119.5 0.1 copy-done.1
  119.6 3.1 %fusion.8 = bf16[2,4,256,512]{3,2,1,0:T(8,128)(2,1)} fusion(bf16[1,384,4,512]{1,3,2,0:T(8,128)(2,1)S(1)} %maximum_bitcast_fusion.10, bf16[1,384,4,512]{1,3,2,0:T(8,128)(2,1)S(1)} %maximum_bitcast_fusion.9, bf16[1,256,2,384]{3,1,2,0:T(8,128)(2,1)S(1)} %copy-done.1, bf16[1,256,2,384]{3,1,2,0:T(8,128)(2,1)S(1)} %copy-done), kind=kOutput, calls=%fused_computation.18 | convolution fusion | flops 1619525632 | bytes 6029312 | tf_op jit(solution)/shard_map/dot_general | solution.py:37
  (23 shorter events, 0.5 us)
Async XLA Ops:
  9.3 11.1 %copy-start.3 = (f32[8,384]{1,0:T(8,128)S(1)}, f32[8,384]{1,0:T(8,128)}, u32[]{:S(2)}) copy-start(f32[8,384]{1,0:T(8,128)} %param.9) | copy-start | bytes 36868
  9.3 11.1 %copy-start.4 = (f32[2,4,384]{2,1,0:T(4,128)S(1)}, f32[2,4,384]{2,1,0:T(4,128)}, u32[]{:S(2)}) copy-start(f32[2,4,384]{2,1,0:T(4,128)} %param.11) | copy-start | bytes 36868
  9.3 11.1 %copy-start.2 = (f32[2,4,4,384]{3,2,1,0:T(4,128)S(1)}, f32[2,4,4,384]{3,2,1,0:T(4,128)}, u32[]{:S(2)}) copy-start(f32[2,4,4,384]{3,2,1,0:T(4,128)} %param.10) | copy-start | bytes 147460
  9.3 61.4 %all-to-all-start = ((bf16[32,2,4,8,512]{4,3,1,2,0:T(8,128)(2,1)}), bf16[32,2,4,8,512]{4,3,1,2,0:T(8,128)(2,1)S(1)}, u32[]{:S(2)}, u32[]{:S(2)}) async-start(bf16[32,2,4,8,512]{4,3,1,2,0:T(8,128)(2,1)} %copy.90), calls=%async_computation | async-start | bytes 4194304 | tf_op jit(solution)/shard_map/all_to_all | solution.py:124
  28.8 1.1 copy-start.5
  70.9 16.1 %collective-permute-start = (bf16[16,2,4,8,512]{4,3,0,1,2:T(8,128)(2,1)S(1)}, bf16[16,2,4,8,512]{4,3,0,1,2:T(8,128)(2,1)S(1)}, u32[]{:S(2)}, u32[]{:S(2)}) collective-permute-start(bf16[16,2,4,8,512]{4,3,0,1,2:T(8,128)(2,1)S(1)} %copy.185), channel_id=1, source_target_pairs={{32,0},{64,32},{96,64},{128,96},{160,128},{192,160},{224,192},{33,... | collective-permute-start | bytes 3145736 | tf_op jit(solution)/shard_map/ppermute | solution.py:16
  88.5 22.5 %collective-permute-start.1 = (bf16[2,384,4,128]{3,1,2,0:T(8,128)(2,1)S(1)}, bf16[2,384,4,128]{3,1,2,0:T(8,128)(2,1)S(1)}, u32[]{:S(2)}, u32[]{:S(2)}) collective-permute-start(bf16[2,384,4,128]{3,1,2,0:T(8,128)(2,1)S(1)} %get-tuple-element.48), channel_id=1, source_target_pairs={{1,0},{2,1},{3,2},{4,3},{5,4},{6,5},{7,6},{8,7},{9,8},{10,9},{11,1... | collective-permute-start | bytes 2359304 | tf_op jit(solution)/shard_map/ppermute | solution.py:16
  118.5 1.0 copy-start
  118.5 1.1 copy-start.1

commit v6 on v5

--- a/solution.py
+++ b/solution.py
@@ -39,7 +39,7 @@
     )
 
 
-def migrate(spectra, border, offsets, tap_weights, block):
+def migrate(window, offsets, tap_weights, block):
     tile = min(128, block)
     taps = tap_weights.shape[0]
     pieces = []
@@ -52,12 +52,7 @@
         onehot = (
             columns[None, None, :] == target[None, :, None] + tap_range[:, None, None]
         ).astype(jnp.bfloat16)
-        if first + tile + MARG <= block:
-            window_part = spectra[:, :, :, first : first + tile + MARG]
-        else:
-            window_part = jnp.concatenate(
-                [spectra[:, :, :, first:], border[:, :, :, :MARG]], axis=3
-            )
+        window_part = window(first, first + tile + MARG)
         picked = lax.dot_general(
             window_part, onehot, (((3,), (2,)), ((), ())), preferred_element_type=jnp.bfloat16
         )
@@ -123,12 +118,39 @@
         )
         turned = lax.all_to_all(result, "dev", 0, 0, tiled=True)
         following = shifted(turned[: dev_count // 2], "blk", -1)
-        spectra = (
-            lax.dot_general(own_table, turned, dims, preferred_element_type=jnp.float32)
-            + lax.dot_general(next_table, following, dims, preferred_element_type=jnp.float32)
+        lead_width = 2 * MARG
+        head = (
+            lax.dot_general(
+                own_table, turned[..., :lead_width], dims, preferred_element_type=jnp.float32
+            )
+            + lax.dot_general(
+                next_table, following[..., :lead_width], dims, preferred_element_type=jnp.float32
+            )
         ).astype(jnp.bfloat16)
-        border = shifted(spectra[:, :, :, : 2 * MARG], "dev", -1)
-        pieces.append(migrate(spectra, border, offsets, tap_weights, block))
+        border = shifted(head, "dev", -1)
+        rest = (
+            lax.dot_general(
+                own_table, turned[..., lead_width:], dims, preferred_element_type=jnp.float32
+            )
+            + lax.dot_general(
+                next_table,
+                following[..., lead_width:],
+                dims,
+                preferred_element_type=jnp.float32,
+            )
+        ).astype(jnp.bfloat16)
+
+        def window(low, high):
+            spans = ((head, 0), (rest, lead_width), (border[..., :MARG], block))
+            parts = []
+            for piece, start in spans:
+                lo = max(low, start)
+                hi = min(high, start + piece.shape[3])
+                if lo < hi:
+                    parts.append(piece[..., lo - start : hi - start])
+            return parts[0] if len(parts) == 1 else jnp.concatenate(parts, axis=3)
+
+        pieces.append(migrate(window, offsets, tap_weights, block))
     moved = jnp.concatenate(pieces, axis=2)
     mix_real = (
         azimuth_filter[0][:, None, :] * channel_mix[0]

time: 123 us -> 123 us (level)
    dot_general x2 -> x4, matrix products: 2.95 us -> 3.45 us  [the longest x1 1.49 us: body(): lax.dot_general(own_table, turned[..., lead_width:], dims, preferred_elem...]
where the time goes in v6:
time: 123 us
  waiting for transfers between devices  62.8 us (51%)
  other arithmetic  22.4 us (18%)
  starting transfers between devices  16.2 us (13%)
  matrix products  15.5 us (13%)
  local copies, waits for them, and re-layouts  5.29 us (4%)
    all_to_all x1, waiting for transfers between devices, body(): turned = lax.all_to_all(result, 'dev', 0, 0, tiled=True)  41.1 us
    ppermute x2, waiting for transfers between devices, shifted(): return lax.ppermute(block, axis, route)  21.7 us
    another operation x15, other arithmetic  12.8 us
    all_to_all x1, starting transfers between devices, body(): turned = lax.all_to_all(result, 'dev', 0, 0, tiled=True)  11 us
    dot_general x4, matrix products, migrate(): lax.dot_general(window_part, onehot, (((3,), (2,)), ((), ())), preferred_...  7.46 us
    ppermute x2, starting transfers between devices, shifted(): return lax.ppermute(block, axis, route)  5.17 us
    add x4, other arithmetic, migrate(): total + picked[:, :, :, tap_index].astype(jnp.float32) * tap_weights[tap_...  5.09 us
    dot_general x2, matrix products, apply_table(): lax.dot_general(table, data, (((2, 3), (part_dim, index_dim)), ((), ())),...  3.87 us
  transfers between devices with their start and end apart: 3, of which 3 were waited for; matrix products, arithmetic and copies ran while one was open for 17% of the time, Pallas kernels for 0%

profile of v6, /device:TPU:27, one launch (start us, length us, event | category | flops | bytes accessed | tf_op | source)
XLA Modules:
  0.0 122.7 jit_solution(4003721978940498949)
XLA Ops:
  0.0 0.3 negate_convert_fusion.2
  0.3 0.3 fusion.104
  0.5 0.3 sine_multiply_fusion.2
  0.8 1.1 fusion.115
  1.9 2.2 %fusion.54 = (bf16[4,8,128,128]{3,1,2,0:T(8,128)(2,1)S(1)}, bf16[4,8,128,128]{3,1,2,0:T(8,128)(2,1)S(1)}) fusion(f32[16384]{0:T(1024)S(1)} %get-tuple-element.54, f32[16384]{0:T(1024)S(1)} %get-tuple-element.53, bf16[2,4,8,16384]{3,2,1,0:T(8,128)(2,1)} %param.6), kind=kLoop, calls=%fused_computation.109 | loop fusion | flops 5242880 | bytes 4325376
  4.1 0.6 copy_bitcast_fusion.3
  4.8 0.7 convolution_bitcast_fusion
  5.5 0.6 subtract_convert_fusion
  6.1 0.7 fusion.12
  6.9 0.8 copy.173
  7.7 1.6 %copy.84 = bf16[32,2,4,8,512]{4,3,1,2,0:T(8,128)(2,1)} copy(bf16[32,2,4,8,512]{4,3,2,1,0:T(8,128)(2,1)S(1)} %bitcast.503) | data formatting | bytes 4194304 | tf_op jit(solution)/shard_map/reshape | solution.py:100
  9.3 11.0 %all-to-all-start = ((bf16[32,2,4,8,512]{4,3,1,2,0:T(8,128)(2,1)}), bf16[32,2,4,8,512]{4,3,1,2,0:T(8,128)(2,1)S(1)}, u32[]{:S(2)}, u32[]{:S(2)}) async-start(bf16[32,2,4,8,512]{4,3,1,2,0:T(8,128)(2,1)} %copy.84), calls=%async_computation | async-start | bytes 4194304 | tf_op jit(solution)/shard_map/all_to_all | solution.py:119
  20.5 1.5 %fusion.86 = bf16[256,1,384]{2,0,1:T(8,128)(2,1)S(1)} fusion(), kind=kLoop, calls=%fused_computation.208 | loop fusion | flops 1081344 | bytes 196608 | tf_op jit(solution)/shard_map/convert.69
  22.1 2.3 %fusion.74 = bf16[384,1,384]{0,2,1:T(8,128)(2,1)S(1)} fusion(), kind=kLoop, calls=%fused_computation.188 | loop fusion | flops 1622016 | bytes 294912 | tf_op jit(solution)/shard_map/convert.61
  24.4 1.7 %negate_convert_fusion.1 = (bf16[256,1,384]{2,0,1:T(8,128)(2,1)S(1)}, bf16[256,1,384]{2,0,1:T(8,128)(2,1)S(1)}) fusion(), kind=kLoop, calls=%fused_computation.201 | loop fusion | flops 1376256 | bytes 393216 | tf_op jit(solution)/shard_map/convert.73
  26.1 2.6 %negate_convert_fusion = (bf16[384,1,384]{0,2,1:T(8,128)(2,1)S(1)}, bf16[384,1,384]{0,2,1:T(8,128)(2,1)S(1)}) fusion(), kind=kLoop, calls=%fused_computation.181 | loop fusion | flops 2064384 | bytes 589824 | tf_op jit(solution)/shard_map/convert.65
  28.7 0.8 maximum_bitcast_fusion.15
  29.6 41.1 %all-to-all-done = bf16[32,2,4,8,512]{4,3,1,2,0:T(8,128)(2,1)S(1)} async-done(((bf16[32,2,4,8,512]{4,3,1,2,0:T(8,128)(2,1)}), bf16[32,2,4,8,512]{4,3,1,2,0:T(8,128)(2,1)S(1)}, u32[]{:S(2)}, u32[]{:S(2)}) %all-to-all-start) | async-done | bytes 2097184 | tf_op jit(solution)/shard_map/all_to_all | solution.py:119
  70.9 2.7 %collective-permute-start = (bf16[16,2,4,8,512]{4,3,0,1,2:T(8,128)(2,1)S(1)}, bf16[16,2,4,8,512]{4,3,0,1,2:T(8,128)(2,1)S(1)}, u32[]{:S(2)}, u32[]{:S(2)}) collective-permute-start(bf16[16,2,4,8,512]{4,3,0,1,2:T(8,128)(2,1)S(1)} %copy.149), channel_id=1, source_target_pairs={{32,0},{64,32},{96,64},{128,96},{160,128},{192,160},{224,192},{33,... | collective-permute-start | bytes 3145736 | tf_op jit(solution)/shard_map/ppermute | solution.py:16
  73.7 0.1 maximum_bitcast_fusion.14
  73.8 0.6 fusion.75
  74.5 1.5 %fusion.15 = f32[2,384,4,384,1,1]{1,3,5,4,2,0:T(8,128)S(1)} fusion(bf16[1,384,2,384]{1,3,2,0:T(8,128)(2,1)S(1)} %get-tuple-element.50, bf16[1,384,2,384]{1,3,2,0:T(8,128)(2,1)S(1)} %get-tuple-element.49, bf16[32,2,4,8,512]{4,3,1,2,0:T(8,128)(2,1)S(1)} %all-to-all-done), kind=kOutput, calls=%fused_computation.31 | convolution fusion | flops 1209532416 | bytes 7471104 | tf_op jit(solution)/shard_map/dot_general | solution.py:132
  76.0 11.1 %collective-permute-done = bf16[16,2,4,8,512]{4,3,0,1,2:T(8,128)(2,1)S(1)} collective-permute-done((bf16[16,2,4,8,512]{4,3,0,1,2:T(8,128)(2,1)S(1)}, bf16[16,2,4,8,512]{4,3,0,1,2:T(8,128)(2,1)S(1)}, u32[]{:S(2)}, u32[]{:S(2)}) %collective-permute-start) | collective-permute-done | bytes 1048608 | tf_op jit(solution)/shard_map/ppermute | solution.py:16
  87.0 0.9 fusion
  88.0 0.4 fusion.44
  88.4 2.5 %collective-permute-start.1 = (bf16[2,384,4,128]{1,3,2,0:T(8,128)(2,1)S(1)}, bf16[2,384,4,128]{1,3,2,0:T(8,128)(2,1)S(1)}, u32[]{:S(2)}, u32[]{:S(2)}) collective-permute-start(bf16[2,384,4,128]{1,3,2,0:T(8,128)(2,1)S(1)} %fusion.44), channel_id=1, source_target_pairs={{1,0},{2,1},{3,2},{4,3},{5,4},{6,5},{7,6},{8,7},{9,8},{10,9},{11,1... | collective-permute-start | bytes 2359304 | tf_op jit(solution)/shard_map/ppermute | solution.py:16
  90.9 1.9 %fusion.45 = bf16[2,384,4,8,128]{1,4,2,0,3:T(8,128)(2,1)S(1)} fusion(bf16[2,384,4,384]{1,3,2,0:T(8,128)(2,1)S(1)} %fusion, s32[8,128]{1,0:T(8,128)S(1)} %get-tuple-element.73), kind=kOutput, calls=%fused_computation.95 | convolution fusion | flops 1208156160 | bytes 7475200 | tf_op jit(solution)/shard_map/dot_general | solution.py:56
  92.8 1.9 %fusion.47 = bf16[2,384,4,8,128]{1,4,3,2,0:T(8,128)(2,1)S(1)} fusion(bf16[2,384,4,64]{1,3,2,0:T(8,128)(2,1)S(1)} %slice.512, bf16[2,384,4,128]{1,3,2,0:T(8,128)(2,1)S(1)} %fusion.44, s32[8,128]{1,0:T(8,128)S(1)} %iota_add_fusion.3), kind=kOutput, calls=%fused_computation.101 | convolution fusion | flops 1210515456 | bytes 7475200 | tf_op jit(solution)/shard_map/dot_general | solution.py:56
  94.7 1.2 fusion.37
  95.9 1.2 fusion.23
  97.1 1.9 %fusion.46 = bf16[2,384,4,8,128]{1,4,2,0,3:T(8,128)(2,1)S(1)} fusion(bf16[2,384,4,384]{1,3,2,0:T(8,128)(2,1)S(1)} %fusion, s32[8,128]{1,0:T(8,128)S(1)} %get-tuple-element.74), kind=kOutput, calls=%fused_computation.97 | convolution fusion | flops 1208156160 | bytes 7475200 | tf_op jit(solution)/shard_map/dot_general | solution.py:56
  99.0 1.2 fusion.30
  100.3 10.7 %collective-permute-done.1 = bf16[2,384,4,128]{1,3,2,0:T(8,128)(2,1)S(1)} collective-permute-done((bf16[2,384,4,128]{1,3,2,0:T(8,128)(2,1)S(1)}, bf16[2,384,4,128]{1,3,2,0:T(8,128)(2,1)S(1)}, u32[]{:S(2)}, u32[]{:S(2)}) %collective-permute-start.1) | collective-permute-done | bytes 786464 | tf_op jit(solution)/shard_map/ppermute | solution.py:16
  111.0 1.9 %fusion.50 = bf16[2,384,4,8,128]{1,4,2,0,3:T(8,128)(2,1)S(1)} fusion(bf16[2,384,4,64]{1,3,2,0:T(8,128)(2,1)S(1)} %slice.540, bf16[2,384,4,128]{1,3,2,0:T(8,128)(2,1)S(1)} %slice-done, s32[8,128]{1,0:T(8,128)S(1)} %iota_add_fusion), kind=kOutput, calls=%fused_computation.105 | convolution fusion | flops 1210515456 | bytes 7475200 | tf_op jit(solution)/shard_map/dot_general | solution.py:56
  112.8 1.4 %fusion.16 = f32[2,384,4,128]{1,3,2,0:T(8,128)S(1)} fusion(bf16[2,384,4,8,128]{1,4,2,0,3:T(8,128)(2,1)S(1)} %fusion.50, f32[384]{0:T(512)S(1)} %get-tuple-element.43, f32[384]{0:T(512)S(1)} %get-tuple-element.44, f32[384]{0:T(512)S(1)} %get-tuple-element.38, f32[384]{0:T(512)S(1)} %get-tuple-element.39, f32[384]{0:T(512)S(1)} %get-tuple-element.40, ...), kind=kLoop, calls=%fused_computation.33 | loop fusion | flops 9043968 | bytes 7876608 | tf_op jit(solution)/shard_map/add | solution.py:61
  114.3 0.5 pad_maximum_fusion
  114.7 0.4 subtract_convert_fusion.3
  115.2 0.4 add_convert_fusion.3
  115.6 0.4 subtract_convert_fusion.4
  116.1 0.4 add_convert_fusion.4
  116.5 0.4 subtract_convert_fusion.2
  117.0 0.4 add_convert_fusion.2
  117.4 0.4 subtract_convert_fusion.1
  117.8 0.4 add_convert_fusion.1
  118.3 0.2 maximum_bitcast_fusion.7
  118.5 0.2 maximum_bitcast_fusion.8
  118.8 0.7 copy-done.1
  119.5 3.2 %fusion.8 = bf16[2,4,256,512]{3,2,1,0:T(8,128)(2,1)} fusion(bf16[1,384,4,512]{1,3,2,0:T(8,128)(2,1)S(1)} %maximum_bitcast_fusion.8, bf16[1,384,4,512]{1,3,2,0:T(8,128)(2,1)S(1)} %maximum_bitcast_fusion.7, bf16[1,256,2,384]{3,1,2,0:T(8,128)(2,1)S(1)} %copy-done.1, bf16[1,256,2,384]{3,1,2,0:T(8,128)(2,1)S(1)} %get-tuple-element.51), kind=kOutput, calls=%fused_computation.18 | convolution fusion | flops 1619525632 | bytes 6029312 | tf_op jit(solution)/shard_map/dot_general | solution.py:37
  (28 shorter events, 0.6 us)
Async XLA Ops:
  9.3 11.0 %copy-start.4 = (f32[2,4,384]{2,1,0:T(4,128)S(1)}, f32[2,4,384]{2,1,0:T(4,128)}, u32[]{:S(2)}) copy-start(f32[2,4,384]{2,1,0:T(4,128)} %param.11) | copy-start | bytes 36868
  9.3 11.1 %copy-start.2 = (f32[2,4,4,384]{3,2,1,0:T(4,128)S(1)}, f32[2,4,4,384]{3,2,1,0:T(4,128)}, u32[]{:S(2)}) copy-start(f32[2,4,4,384]{3,2,1,0:T(4,128)} %param.10) | copy-start | bytes 147460
  9.3 61.4 %all-to-all-start = ((bf16[32,2,4,8,512]{4,3,1,2,0:T(8,128)(2,1)}), bf16[32,2,4,8,512]{4,3,1,2,0:T(8,128)(2,1)S(1)}, u32[]{:S(2)}, u32[]{:S(2)}) async-start(bf16[32,2,4,8,512]{4,3,1,2,0:T(8,128)(2,1)} %copy.84), calls=%async_computation | async-start | bytes 4194304 | tf_op jit(solution)/shard_map/all_to_all | solution.py:119
  20.3 9.3 %copy-start.5 = (s32[512]{0:T(512)S(1)}, s32[512]{0:T(512)}, u32[]{:S(2)}) copy-start(s32[512]{0:T(512)} %param.8) | copy-start | bytes 6148
  70.8 2.8 %copy-start.3 = (f32[8,384]{1,0:T(8,128)S(1)}, f32[8,384]{1,0:T(8,128)}, u32[]{:S(2)}) copy-start(f32[8,384]{1,0:T(8,128)} %param.9) | copy-start | bytes 36868
  70.9 16.1 %collective-permute-start = (bf16[16,2,4,8,512]{4,3,0,1,2:T(8,128)(2,1)S(1)}, bf16[16,2,4,8,512]{4,3,0,1,2:T(8,128)(2,1)S(1)}, u32[]{:S(2)}, u32[]{:S(2)}) collective-permute-start(bf16[16,2,4,8,512]{4,3,0,1,2:T(8,128)(2,1)S(1)} %copy.149), channel_id=1, source_target_pairs={{32,0},{64,32},{96,64},{128,96},{160,128},{192,160},{224,192},{33,... | collective-permute-start | bytes 3145736 | tf_op jit(solution)/shard_map/ppermute | solution.py:16
  87.9 9.2 %copy-start = (bf16[2,384,4,384]{1,3,2,0:T(8,128)(2,1)}, bf16[2,384,4,384]{1,3,2,0:T(8,128)(2,1)S(1)}, u32[]{:S(2)}) copy-start(bf16[2,384,4,384]{1,3,2,0:T(8,128)(2,1)S(1)} %fusion) | copy-start | bytes 7077892
  88.4 22.5 %collective-permute-start.1 = (bf16[2,384,4,128]{1,3,2,0:T(8,128)(2,1)S(1)}, bf16[2,384,4,128]{1,3,2,0:T(8,128)(2,1)S(1)}, u32[]{:S(2)}, u32[]{:S(2)}) collective-permute-start(bf16[2,384,4,128]{1,3,2,0:T(8,128)(2,1)S(1)} %fusion.44), channel_id=1, source_target_pairs={{1,0},{2,1},{3,2},{4,3},{5,4},{6,5},{7,6},{8,7},{9,8},{10,9},{11,1... | collective-permute-start | bytes 2359304 | tf_op jit(solution)/shard_map/ppermute | solution.py:16
  99.0 11.9 %slice-start = ((bf16[2,384,4,384]{1,3,2,0:T(8,128)(2,1)}), bf16[2,384,4,128]{1,3,2,0:T(8,128)(2,1)S(1)}, s32[]{:S(2)}) async-start(bf16[2,384,4,384]{1,3,2,0:T(8,128)(2,1)} %copy-done), calls=%async_computation.1 | async-start | bytes 1572864 | tf_op jit(solution)/shard_map/slice | solution.py:150
  118.5 1.0 copy-start.1

commit v7 on v6

--- a/solution.py
+++ b/solution.py
@@ -62,7 +62,7 @@
                 tap_index
             ][None, :, None, None]
         pieces.append(total)
-    return jnp.concatenate(pieces, axis=3)
+    return pieces
 
 
 CHUNKS = 1
@@ -151,7 +151,7 @@
             return parts[0] if len(parts) == 1 else jnp.concatenate(parts, axis=3)
 
         pieces.append(migrate(window, offsets, tap_weights, block))
-    moved = jnp.concatenate(pieces, axis=2)
+    tiles_moved = [jnp.concatenate(group, axis=2) for group in zip(*pieces)]
     mix_real = (
         azimuth_filter[0][:, None, :] * channel_mix[0]
         - azimuth_filter[1][:, None, :] * channel_mix[1]
@@ -160,25 +160,35 @@
         azimuth_filter[0][:, None, :] * channel_mix[1]
         + azimuth_filter[1][:, None, :] * channel_mix[0]
     )
-    rows_real = []
-    rows_imag = []
-    for channel in range(channels):
-        sum_real = jnp.zeros((wide, block), jnp.float32)
-        sum_imag = jnp.zeros((wide, block), jnp.float32)
-        for other_chan in range(channels):
-            coef_real = mix_real[channel, other_chan][:, None]
-            coef_imag = mix_imag[channel, other_chan][:, None]
-            sum_real = (
-                sum_real + coef_real * moved[0, :, other_chan] - coef_imag * moved[1, :, other_chan]
-            )
-            sum_imag = (
-                sum_imag + coef_real * moved[1, :, other_chan] + coef_imag * moved[0, :, other_chan]
-            )
-        rows_real.append(sum_real)
-        rows_imag.append(sum_imag)
-    focused = jnp.stack([jnp.stack(rows_real, axis=1), jnp.stack(rows_imag, axis=1)]).astype(
-        jnp.bfloat16
-    )
+    focused_tiles = []
+    for moved in tiles_moved:
+        width = moved.shape[3]
+        rows_real = []
+        rows_imag = []
+        for channel in range(channels):
+            sum_real = jnp.zeros((wide, width), jnp.float32)
+            sum_imag = jnp.zeros((wide, width), jnp.float32)
+            for other_chan in range(channels):
+                coef_real = mix_real[channel, other_chan][:, None]
+                coef_imag = mix_imag[channel, other_chan][:, None]
+                sum_real = (
+                    sum_real
+                    + coef_real * moved[0, :, other_chan]
+                    - coef_imag * moved[1, :, other_chan]
+                )
+                sum_imag = (
+                    sum_imag
+                    + coef_real * moved[1, :, other_chan]
+                    + coef_imag * moved[0, :, other_chan]
+                )
+            rows_real.append(sum_real)
+            rows_imag.append(sum_imag)
+        focused_tiles.append(
+            jnp.stack([jnp.stack(rows_real, axis=1), jnp.stack(rows_imag, axis=1)]).astype(
+                jnp.bfloat16
+            )
+        )
+    focused = jnp.concatenate(focused_tiles, axis=3)
     backward = complex_table(group_pulses, wide, wide, 1.0, 1.0 / math.sqrt(wide))
     image = apply_table(backward, focused, 0, 1).astype(jnp.bfloat16)
     return image.transpose(0, 2, 1, 3)

time: 123 us -> 131 us (1.065)
  waiting for transfers between devices: 62.8 us -> 71.4 us
    ppermute x2, waiting for transfers between devices: 21.7 us -> 30.3 us  [shifted(): return lax.ppermute(block, axis, route)]
    another operation x15 -> x39, other arithmetic: 12.8 us -> 13.1 us
  transfers between devices with their start and end apart: 3 -> 3, of which waited for: 3 -> 3; matrix products, arithmetic and copies ran while one was open for 17% -> 9% of each run, Pallas kernels for 0% -> 0%
where the time goes in v7:
time: 131 us
  waiting for transfers between devices  71.4 us (55%)
  other arithmetic  22 us (17%)
  starting transfers between devices  16.2 us (12%)
  matrix products  15.6 us (12%)
  local copies, waits for them, and re-layouts  5.28 us (4%)
    all_to_all x1, waiting for transfers between devices, body(): turned = lax.all_to_all(result, 'dev', 0, 0, tiled=True)  41.1 us
    ppermute x2, waiting for transfers between devices, shifted(): return lax.ppermute(block, axis, route)  30.3 us
    another operation x39, other arithmetic  13.1 us
    all_to_all x1, starting transfers between devices, body(): turned = lax.all_to_all(result, 'dev', 0, 0, tiled=True)  11 us
    dot_general x4, matrix products, migrate(): lax.dot_general(window_part, onehot, (((3,), (2,)), ((), ())), preferred_...  7.7 us
    ppermute x2, starting transfers between devices, shifted(): return lax.ppermute(block, axis, route)  5.17 us
    add x4, other arithmetic, migrate(): total + picked[:, :, :, tap_index].astype(jnp.float32) * tap_weights[tap_...  4.85 us
    dot_general x2, matrix products, apply_table(): lax.dot_general(table, data, (((2, 3), (part_dim, index_dim)), ((), ())),...  3.75 us
  transfers between devices with their start and end apart: 3, of which 3 were waited for; matrix products, arithmetic and copies ran while one was open for 9% of the time, Pallas kernels for 0%

profile of v7, /device:TPU:27, one launch (start us, length us, event | category | flops | bytes accessed | tf_op | source)
XLA Modules:
  0.0 130.9 jit_solution(6766928953424729087)
XLA Ops:
  0.0 0.3 negate_convert_fusion.2
  0.3 0.3 fusion.116
  0.5 0.3 sine_multiply_fusion.2
  0.8 1.1 fusion.127
  1.9 2.2 %fusion.66 = (bf16[4,8,128,128]{3,1,2,0:T(8,128)(2,1)S(1)}, bf16[4,8,128,128]{3,1,2,0:T(8,128)(2,1)S(1)}) fusion(f32[16384]{0:T(1024)S(1)} %get-tuple-element.54, f32[16384]{0:T(1024)S(1)} %get-tuple-element.53, bf16[2,4,8,16384]{3,2,1,0:T(8,128)(2,1)} %param.6), kind=kLoop, calls=%fused_computation.118 | loop fusion | flops 5242880 | bytes 4325376
  4.1 0.6 copy_bitcast_fusion.3
  4.8 0.7 convolution_bitcast_fusion
  5.5 0.6 subtract_convert_fusion
  6.1 0.7 fusion.24
  6.9 0.8 copy.173
  7.7 1.6 %copy.84 = bf16[32,2,4,8,512]{4,3,1,2,0:T(8,128)(2,1)} copy(bf16[32,2,4,8,512]{4,3,2,1,0:T(8,128)(2,1)S(1)} %bitcast.947) | data formatting | bytes 4194304 | tf_op jit(solution)/shard_map/reshape | solution.py:100
  9.3 11.0 %all-to-all-start = ((bf16[32,2,4,8,512]{4,3,1,2,0:T(8,128)(2,1)}), bf16[32,2,4,8,512]{4,3,1,2,0:T(8,128)(2,1)S(1)}, u32[]{:S(2)}, u32[]{:S(2)}) async-start(bf16[32,2,4,8,512]{4,3,1,2,0:T(8,128)(2,1)} %copy.84), calls=%async_computation | async-start | bytes 4194304 | tf_op jit(solution)/shard_map/all_to_all | solution.py:119
  20.5 1.5 %fusion.98 = bf16[256,1,384]{2,0,1:T(8,128)(2,1)S(1)} fusion(), kind=kLoop, calls=%fused_computation.209 | loop fusion | flops 1081344 | bytes 196608 | tf_op jit(solution)/shard_map/convert.105
  22.1 2.3 %fusion.86 = bf16[384,1,384]{0,2,1:T(8,128)(2,1)S(1)} fusion(), kind=kLoop, calls=%fused_computation.181 | loop fusion | flops 1622016 | bytes 294912 | tf_op jit(solution)/shard_map/convert.97
  24.4 1.7 %negate_convert_fusion.1 = (bf16[256,1,384]{2,0,1:T(8,128)(2,1)S(1)}, bf16[256,1,384]{2,0,1:T(8,128)(2,1)S(1)}) fusion(), kind=kLoop, calls=%fused_computation.202 | loop fusion | flops 1376256 | bytes 393216 | tf_op jit(solution)/shard_map/convert.109
  26.1 2.6 %negate_convert_fusion = (bf16[384,1,384]{0,2,1:T(8,128)(2,1)S(1)}, bf16[384,1,384]{0,2,1:T(8,128)(2,1)S(1)}) fusion(), kind=kLoop, calls=%fused_computation.174 | loop fusion | flops 2064384 | bytes 589824 | tf_op jit(solution)/shard_map/convert.101
  28.7 0.8 maximum_bitcast_fusion.13
  29.6 41.1 %all-to-all-done = bf16[32,2,4,8,512]{4,3,1,2,0:T(8,128)(2,1)S(1)} async-done(((bf16[32,2,4,8,512]{4,3,1,2,0:T(8,128)(2,1)}), bf16[32,2,4,8,512]{4,3,1,2,0:T(8,128)(2,1)S(1)}, u32[]{:S(2)}, u32[]{:S(2)}) %all-to-all-start) | async-done | bytes 2097184 | tf_op jit(solution)/shard_map/all_to_all | solution.py:119
  70.9 2.7 %collective-permute-start = (bf16[16,2,4,8,512]{4,3,0,1,2:T(8,128)(2,1)S(1)}, bf16[16,2,4,8,512]{4,3,0,1,2:T(8,128)(2,1)S(1)}, u32[]{:S(2)}, u32[]{:S(2)}) collective-permute-start(bf16[16,2,4,8,512]{4,3,0,1,2:T(8,128)(2,1)S(1)} %copy.149), channel_id=1, source_target_pairs={{32,0},{64,32},{96,64},{128,96},{160,128},{192,160},{224,192},{33,... | collective-permute-start | bytes 3145736 | tf_op jit(solution)/shard_map/ppermute | solution.py:16
  73.7 0.1 maximum_bitcast_fusion.12
  73.8 0.6 fusion.87
  74.5 1.5 %fusion.27 = f32[2,384,4,384,1,1]{1,3,5,4,2,0:T(8,128)S(1)} fusion(bf16[1,384,2,384]{1,3,2,0:T(8,128)(2,1)S(1)} %get-tuple-element.50, bf16[1,384,2,384]{1,3,2,0:T(8,128)(2,1)S(1)} %get-tuple-element.49, bf16[32,2,4,8,512]{4,3,1,2,0:T(8,128)(2,1)S(1)} %all-to-all-done), kind=kOutput, calls=%fused_computation.40 | convolution fusion | flops 1209532416 | bytes 7471104 | tf_op jit(solution)/shard_map/dot_general | solution.py:132
  76.0 11.1 %collective-permute-done = bf16[16,2,4,8,512]{4,3,0,1,2:T(8,128)(2,1)S(1)} collective-permute-done((bf16[16,2,4,8,512]{4,3,0,1,2:T(8,128)(2,1)S(1)}, bf16[16,2,4,8,512]{4,3,0,1,2:T(8,128)(2,1)S(1)}, u32[]{:S(2)}, u32[]{:S(2)}) %collective-permute-start) | collective-permute-done | bytes 1048608 | tf_op jit(solution)/shard_map/ppermute | solution.py:16
  87.0 0.9 fusion
  88.0 0.4 fusion.56
  88.4 1.9 %fusion.59 = bf16[2,384,4,8,128]{1,4,3,2,0:T(8,128)(2,1)S(1)} fusion(bf16[2,384,4,64]{1,3,2,0:T(8,128)(2,1)S(1)} %slice.394, bf16[2,384,4,128]{1,3,2,0:T(8,128)(2,1)S(1)} %fusion.56, s32[8,128]{1,0:T(8,128)S(1)} %iota_add_fusion.3), kind=kOutput, calls=%fused_computation.110 | convolution fusion | flops 1210515456 | bytes 7475200 | tf_op jit(solution)/shard_map/dot_general | solution.py:56
  90.3 1.2 fusion.49
  91.5 0.1 subtract_convert_fusion.13
  91.6 0.1 add_convert_fusion.13
  91.9 0.1 add_convert_fusion.14
  92.1 0.1 add_convert_fusion.15
  92.5 1.9 %fusion.58 = bf16[2,384,4,8,128]{1,4,2,0,3:T(8,128)(2,1)S(1)} fusion(bf16[2,384,4,384]{1,3,2,0:T(8,128)(2,1)S(1)} %fusion, s32[8,128]{1,0:T(8,128)S(1)} %get-tuple-element.74), kind=kOutput, calls=%fused_computation.106 | convolution fusion | flops 1208156160 | bytes 7475200 | tf_op jit(solution)/shard_map/dot_general | solution.py:56
  94.3 1.2 fusion.42
  95.6 0.1 subtract_convert_fusion.10
  96.0 0.1 add_convert_fusion.10
  96.5 2.1 %fusion.57 = bf16[2,384,4,8,128]{1,4,2,0,3:T(8,128)(2,1)S(1)} fusion(bf16[2,384,4,384]{1,3,2,0:T(8,128)(2,1)S(1)} %fusion, s32[8,128]{1,0:T(8,128)S(1)} %get-tuple-element.73), kind=kOutput, calls=%fused_computation.104 | convolution fusion | flops 1208156160 | bytes 7475200 | tf_op jit(solution)/shard_map/dot_general | solution.py:56
  98.6 1.2 fusion.35
  99.8 0.1 subtract_convert_fusion.5
  100.4 2.5 %collective-permute-start.1 = (bf16[2,384,4,128]{1,3,2,0:T(8,128)(2,1)S(1)}, bf16[2,384,4,128]{1,3,2,0:T(8,128)(2,1)S(1)}, u32[]{:S(2)}, u32[]{:S(2)}) collective-permute-start(bf16[2,384,4,128]{1,3,2,0:T(8,128)(2,1)S(1)} %fusion.56), channel_id=1, source_target_pairs={{1,0},{2,1},{3,2},{4,3},{5,4},{6,5},{7,6},{8,7},{9,8},{10,9},{11,1... | collective-permute-start | bytes 2359304 | tf_op jit(solution)/shard_map/ppermute | solution.py:16
  103.3 0.1 add_convert_fusion.6
  103.7 19.2 %collective-permute-done.1 = bf16[2,384,4,128]{1,3,2,0:T(8,128)(2,1)S(1)} collective-permute-done((bf16[2,384,4,128]{1,3,2,0:T(8,128)(2,1)S(1)}, bf16[2,384,4,128]{1,3,2,0:T(8,128)(2,1)S(1)}, u32[]{:S(2)}, u32[]{:S(2)}) %collective-permute-start.1) | collective-permute-done | bytes 786464 | tf_op jit(solution)/shard_map/ppermute | solution.py:16
  123.0 1.9 %fusion.62 = bf16[2,384,4,8,128]{1,4,2,0,3:T(8,128)(2,1)S(1)} fusion(bf16[2,384,4,64]{1,3,2,0:T(8,128)(2,1)S(1)} %slice.477, bf16[2,384,4,128]{1,3,2,0:T(8,128)(2,1)S(1)} %slice-done, s32[8,128]{1,0:T(8,128)S(1)} %iota_add_fusion), kind=kOutput, calls=%fused_computation.114 | convolution fusion | flops 1210515456 | bytes 7475200 | tf_op jit(solution)/shard_map/dot_general | solution.py:56
  124.8 1.2 fusion.28
  126.0 0.1 subtract_convert_fusion.1
  126.6 0.1 add_convert_fusion.3
  126.9 0.1 add_convert_fusion.1
  127.1 0.7 copy-done.1
  127.9 3.0 %fusion.20 = bf16[2,4,256,512]{3,2,1,0:T(8,128)(2,1)} fusion(bf16[1,384,4,128]{1,3,2,0:T(8,128)(2,1)S(1)} %maximum_bitcast_fusion.22, bf16[1,384,4,128]{1,3,2,0:T(8,128)(2,1)S(1)} %maximum_bitcast_fusion.21, bf16[1,384,4,128]{1,3,2,0:T(8,128)(2,1)S(1)} %maximum_bitcast_fusion.20, bf16[1,384,4,128]{1,3,2,0:T(8,128)(2,1)S(1)} %maximum_bitcast_fusion.19, ...), kind=kOutput, calls=%fused_computation.29 | convolution fusion | flops 1638400000 | bytes 6029312 | tf_op jit(solution)/shard_map/dot_general | solution.py:37
  (57 shorter events, 3.5 us)
Async XLA Ops:
  9.3 11.0 %copy-start.4 = (f32[2,4,384]{2,1,0:T(4,128)S(1)}, f32[2,4,384]{2,1,0:T(4,128)}, u32[]{:S(2)}) copy-start(f32[2,4,384]{2,1,0:T(4,128)} %param.11) | copy-start | bytes 36868
  9.3 11.1 %copy-start.2 = (f32[2,4,4,384]{3,2,1,0:T(4,128)S(1)}, f32[2,4,4,384]{3,2,1,0:T(4,128)}, u32[]{:S(2)}) copy-start(f32[2,4,4,384]{3,2,1,0:T(4,128)} %param.10) | copy-start | bytes 147460
  9.3 61.4 %all-to-all-start = ((bf16[32,2,4,8,512]{4,3,1,2,0:T(8,128)(2,1)}), bf16[32,2,4,8,512]{4,3,1,2,0:T(8,128)(2,1)S(1)}, u32[]{:S(2)}, u32[]{:S(2)}) async-start(bf16[32,2,4,8,512]{4,3,1,2,0:T(8,128)(2,1)} %copy.84), calls=%async_computation | async-start | bytes 4194304 | tf_op jit(solution)/shard_map/all_to_all | solution.py:119
  20.3 9.3 %copy-start.5 = (s32[512]{0:T(512)S(1)}, s32[512]{0:T(512)}, u32[]{:S(2)}) copy-start(s32[512]{0:T(512)} %param.8) | copy-start | bytes 6148
  70.8 2.8 %copy-start.3 = (f32[8,384]{1,0:T(8,128)S(1)}, f32[8,384]{1,0:T(8,128)}, u32[]{:S(2)}) copy-start(f32[8,384]{1,0:T(8,128)} %param.9) | copy-start | bytes 36868
  70.9 16.1 %collective-permute-start = (bf16[16,2,4,8,512]{4,3,0,1,2:T(8,128)(2,1)S(1)}, bf16[16,2,4,8,512]{4,3,0,1,2:T(8,128)(2,1)S(1)}, u32[]{:S(2)}, u32[]{:S(2)}) collective-permute-start(bf16[16,2,4,8,512]{4,3,0,1,2:T(8,128)(2,1)S(1)} %copy.149), channel_id=1, source_target_pairs={{32,0},{64,32},{96,64},{128,96},{160,128},{192,160},{224,192},{33,... | collective-permute-start | bytes 3145736 | tf_op jit(solution)/shard_map/ppermute | solution.py:16
  87.9 12.5 %copy-start = (bf16[2,384,4,384]{1,3,2,0:T(8,128)(2,1)}, bf16[2,384,4,384]{1,3,2,0:T(8,128)(2,1)S(1)}, u32[]{:S(2)}) copy-start(bf16[2,384,4,384]{1,3,2,0:T(8,128)(2,1)S(1)} %fusion) | copy-start | bytes 7077892
  100.4 22.5 %collective-permute-start.1 = (bf16[2,384,4,128]{1,3,2,0:T(8,128)(2,1)S(1)}, bf16[2,384,4,128]{1,3,2,0:T(8,128)(2,1)S(1)}, u32[]{:S(2)}, u32[]{:S(2)}) collective-permute-start(bf16[2,384,4,128]{1,3,2,0:T(8,128)(2,1)S(1)} %fusion.56), channel_id=1, source_target_pairs={{1,0},{2,1},{3,2},{4,3},{5,4},{6,5},{7,6},{8,7},{9,8},{10,9},{11,1... | collective-permute-start | bytes 2359304 | tf_op jit(solution)/shard_map/ppermute | solution.py:16
  103.5 19.4 %slice-start = ((bf16[2,384,4,384]{1,3,2,0:T(8,128)(2,1)}), bf16[2,384,4,128]{1,3,2,0:T(8,128)(2,1)S(1)}, s32[]{:S(2)}) async-start(bf16[2,384,4,384]{1,3,2,0:T(8,128)(2,1)} %copy-done), calls=%async_computation.1 | async-start | bytes 1572864 | tf_op jit(solution)/shard_map/slice | solution.py:150
  126.9 1.0 copy-start.1
